TPU v7x, 512 devices: a whole 4x8x8 slice. The times are simulated.
512 devices in a mesh: section: 2 (over z_lo), tensor: 4 (over x), seq: 64 (over y, z_hi, core).
Axes of the slice: x: 4, y: 8, z: 8 (z_hi: 4, z_lo: 2; z = z_hi * 2 + z_lo), core: 2. Of those that a mesh axis runs over, the one named last changes fastest.
Arguments:
- tokens: bfloat16 [16384, 2560], P('seq', ('section', 'tensor')), may hold values from -6 to 6
- w_query: bfloat16 [2560, 2048], P(None, ('section', 'tensor')), may hold values from -0.125 to 0.125
- w_keyval: bfloat16 [2560, 2048], P(None, ('section', 'tensor')), may hold values from -0.125 to 0.125
- w_out: bfloat16 [2048, 2560], P(('section', 'tensor')), may hold values from -0.125 to 0.125
- w_gateup: bfloat16 [2560, 2, 5120], P('seq', None, ('section', 'tensor')), may hold values from -0.125 to 0.125
- attn_gain: float32 [2560], replicated, may hold values from 0.1 to 1.9
- post_gain: float32 [2560], replicated, may hold values from 0.1 to 1.9
- mlp_gain: float32 [2560], replicated, may hold values from 0.1 to 1.9
- query_gain: float32 [256], replicated, may hold values from 0.7 to 6.5
- key_gain: float32 [256], replicated, may hold values from 0.7 to 6.5
- prompt_lengths: int32 [8], replicated, may hold values from 1 to 4096, as said below
- page_slots: int32 [128], P('seq'), may hold values from 0 to 1, as said below
Outputs:
- hidden: bfloat16 [16384, 5120], P('seq', ('section', 'tensor'))
- page_cache: bfloat16 [128, 128, 2048], P('seq', None, ('section', 'tensor'))
Inputs may be any that keep to these rules, and one draw needn't show every extreme that they name: `prompt_lengths`: each prompt has at least one token; they sum to 16384; one prompt has exactly 4096 tokens and begins strictly inside a token block. `page_slots`: within each aligned group of 2 pages (the pages of one token block) the slots are a permutation of 0 to 1.
All inputs are finite; a program needn't handle non-finite values.
Results may differ from a plain program's by a relative error of at most 0.01.
The roundings to bfloat16 on the way count: a program that leaves them out, or rounds other values in their place, can miss the bound.
Values may be sent and summed in bfloat16 or wider, within the bound.
No kernel may reach another device: no remote copies, remote signals or barrier semaphores. Data moves between devices by JAX's collectives and lax.ppermute only.
A program may use at most 64 MiB of HBM per device.

v0:
```python
import jax
import jax.numpy as jnp
from jax import lax
from jax.sharding import PartitionSpec as P

REACH = 16


NORM_EPS = 1e-06
ROPE_BASE = 1000000.0
ROPE_FACTOR = 8.0


def swapped(value, axis, bit):
    mask = 2**bit
    pairs = [(source, source ^ mask) for source in range(lax.axis_size(axis))]
    return lax.ppermute(value, axis, pairs)


def shifted(block, axis, distance):
    devices = range(lax.axis_size(axis))
    route = [(i - distance, i) for i in devices if i - distance in devices]
    return lax.ppermute(block, axis, route)


GROUP = ("section", "tensor")


def group_count():
    return lax.axis_size("section") * lax.axis_size("tensor")


def group_parts(value):
    spread = jnp.broadcast_to(value[None], (group_count(),) + value.shape)
    return lax.all_to_all(spread, GROUP, 0, 0, tiled=True)


def group_gather(block):
    rows, width = block.shape
    parts = group_parts(block)
    return parts.transpose(1, 0, 2).reshape(rows, parts.shape[0] * width)


def group_sum(vector):
    return jnp.sum(group_parts(vector), axis=0)


def rms_norm(values, weights):
    values = values.astype(jnp.float32)
    inverse = lax.rsqrt(jnp.mean(values * values, axis=-1, keepdims=True) + NORM_EPS)
    return values * inverse * weights


def angle_tables(position, head_width):
    halfway = head_width // 2
    exponent = jnp.arange(halfway, dtype=jnp.float32) * (2.0 / head_width)
    frequency = ROPE_BASE ** (-exponent)
    angles = (position.astype(jnp.float32) / ROPE_FACTOR)[:, None] * frequency[None, :]
    return (jnp.cos(angles), jnp.sin(angles))


def rotary(values, cosine_table, sine_table):
    halfway = values.shape[-1] // 2
    lower_half = values[..., :halfway]
    upper_half = values[..., halfway:]
    return jnp.concatenate(
        [
            lower_half * cosine_table - upper_half * sine_table,
            upper_half * cosine_table + lower_half * sine_table,
        ],
        axis=-1,
    )


def local(
    tokens,
    w_query,
    w_keyval,
    w_out,
    w_gateup,
    attn_gain,
    post_gain,
    mlp_gain,
    query_gain,
    key_gain,
    prompt_lengths,
    page_slots,
):
    row_count = tokens.shape[0]
    head_width = w_query.shape[1]
    halfway = head_width // 2
    unit_count = w_gateup.shape[2]
    span_blocks = min(REACH, lax.axis_size("seq") // 2)
    features = group_gather(tokens)
    out_columns = lax.all_to_all(w_out, GROUP, 1, 0, tiled=True)
    first_row = lax.axis_index("seq") * row_count
    prompt_ends = jnp.cumsum(prompt_lengths)
    prompt_starts = prompt_ends - prompt_lengths
    query_index = first_row + jnp.arange(row_count, dtype=jnp.int32)
    query_segment = jnp.sum(
        (prompt_ends[None, :] <= query_index[:, None]).astype(jnp.int32), axis=1
    )
    chosen = query_segment[:, None] == jnp.arange(prompt_ends.shape[0], dtype=jnp.int32)[None, :]
    query_position = query_index - jnp.sum(jnp.where(chosen, prompt_starts[None, :], 0), axis=1)
    cosine_table, sine_table = angle_tables(query_position, head_width)
    normed = rms_norm(features, attn_gain).astype(jnp.bfloat16)
    queries = jnp.dot(normed, w_query, preferred_element_type=jnp.float32)
    queries = rotary(rms_norm(queries, query_gain), cosine_table, sine_table).astype(jnp.bfloat16)
    own_half = jnp.dot(normed, w_keyval, preferred_element_type=jnp.float32).astype(jnp.bfloat16)
    other_half = swapped(own_half, "tensor", 0)
    is_lower = lax.axis_index("tensor") % 2 == 0
    lower_part = jnp.where(is_lower, own_half, other_half)
    upper_part = jnp.where(is_lower, other_half, own_half)
    raw_keys = jnp.concatenate([lower_part[:, :halfway], upper_part[:, :halfway]], axis=1)
    values_full = jnp.concatenate([lower_part[:, halfway:], upper_part[:, halfway:]], axis=1)
    keys_full = rotary(rms_norm(raw_keys, key_gain), cosine_table, sine_table).astype(jnp.bfloat16)
    own_keys = jnp.where(is_lower, keys_full[:, :halfway], keys_full[:, halfway:])
    page_rows = jnp.concatenate([own_keys, own_half[:, halfway:]], axis=1)
    pages_here = page_slots.shape[0]
    page_rows = page_rows.reshape(pages_here, row_count // pages_here, head_width)
    page_cache = jnp.zeros_like(page_rows).at[page_slots].set(page_rows)
    key_block = jnp.stack([keys_full, values_full])
    half_span = span_blocks // 2
    series = key_block[None]
    while series.shape[0] < half_span:
        received = shifted(series, "seq", 2 * series.shape[0])
        series = jnp.concatenate([series, received], axis=0)
    series = jnp.concatenate([series, shifted(key_block, "seq", 2 * half_span)[None]], axis=0)
    partner = swapped(series, "seq", 0)
    parity = lax.axis_index("seq") % 2
    odd = lax.dynamic_slice_in_dim(partner, 1 - parity, half_span, axis=0)
    window_stack = jnp.concatenate([series, odd], axis=0)
    all_keys = window_stack[:, 0].reshape(-1, head_width)
    all_values = window_stack[:, 1].reshape(-1, head_width)
    distances = list(range(0, 2 * half_span + 1, 2)) + list(range(1, 2 * half_span, 2))
    offsets = (jnp.array(distances, dtype=jnp.int32) * row_count)[:, None]
    key_index = (first_row - offsets + jnp.arange(row_count, dtype=jnp.int32)[None, :]).reshape(-1)
    key_segment = jnp.sum((prompt_ends[None, :] <= key_index[:, None]).astype(jnp.int32), axis=1)
    key_segment = jnp.where(key_index >= 0, key_segment, -1)
    allowed = (key_segment[None, :] == query_segment[:, None]) & (
        key_index[None, :] <= query_index[:, None]
    )
    scores = lax.dot_general(
        queries, all_keys, (((1,), (1,)), ((), ())), preferred_element_type=jnp.float32
    ) * head_width ** (-0.5)
    scores = jnp.where(allowed, scores, -jnp.inf)
    row_max = jnp.max(scores, axis=1, keepdims=True)
    exponent_terms = jnp.exp(scores - row_max)
    weights_low = (exponent_terms / jnp.sum(exponent_terms, axis=1, keepdims=True)).astype(
        jnp.bfloat16
    )
    attention_out = jnp.dot(weights_low, all_values, preferred_element_type=jnp.float32).astype(
        jnp.bfloat16
    )
    all_heads = group_gather(attention_out)
    attended = jnp.dot(all_heads, out_columns, preferred_element_type=jnp.float32)
    width = attended.shape[1]
    first_column = lax.axis_index(GROUP) * width
    post_local = lax.dynamic_slice_in_dim(post_gain, first_column, width)
    mlp_local = lax.dynamic_slice_in_dim(mlp_gain, first_column, width)
    model_width = features.shape[1]
    token_rows = tokens.astype(jnp.float32)
    scaled = attended * post_local
    sums = group_sum(
        jnp.stack(
            [
                jnp.sum(attended * attended, axis=1),
                jnp.sum(token_rows * token_rows, axis=1),
                jnp.sum(token_rows * scaled, axis=1),
                jnp.sum(scaled * scaled, axis=1),
            ]
        )
    )
    attended_inverse = lax.rsqrt(sums[0] / model_width + NORM_EPS)
    residual = token_rows + attended * attended_inverse[:, None] * post_local
    residual_square = jnp.maximum(
        sums[1] + 2.0 * attended_inverse * sums[2] + attended_inverse * attended_inverse * sums[3],
        0.0,
    )
    residual_inverse = lax.rsqrt(residual_square / model_width + NORM_EPS)
    ffn_local = (residual * residual_inverse[:, None] * mlp_local).astype(jnp.bfloat16)
    ffn_input = group_gather(ffn_local)
    row_piece = lax.all_gather(
        w_gateup.reshape(w_gateup.shape[0], 2 * unit_count), "seq", axis=0, tiled=True
    )
    projected = jnp.dot(ffn_input, row_piece, preferred_element_type=jnp.float32)
    hidden = (
        jax.nn.gelu(projected[:, :unit_count], approximate=True) * projected[:, unit_count:]
    ).astype(jnp.bfloat16)
    return (hidden, page_cache)


def solution(mesh):
    return jax.shard_map(
        local,
        mesh=mesh,
        in_specs=(
            P("seq", ("section", "tensor")),
            P(None, ("section", "tensor")),
            P(None, ("section", "tensor")),
            P(("section", "tensor"), None),
            P("seq", None, ("section", "tensor")),
            P(),
            P(),
            P(),
            P(),
            P(),
            P(),
            P("seq"),
        ),
        out_specs=(P("seq", ("section", "tensor")), P("seq", None, ("section", "tensor"))),
        check_vma=False,
    )
```

profile of v0, /device:TPU:48, one launch (start us, length us, event | category | flops | bytes accessed | tf_op | source)
XLA Modules:
  0.0 274.0 jit_solution(8794560125186487310)
XLA Ops:
  9.4 6.2 %all-to-all-start = ((bf16[8,256,320]{1,2,0:T(8,128)(2,1)}), bf16[8,256,320]{1,2,0:T(8,128)(2,1)S(1)}, u32[]{:S(2)}, u32[]{:S(2)}) async-start(bf16[8,256,320]{1,2,0:T(8,128)(2,1)} %broadcast_in_dim.36), calls=%async_computation | async-start | bytes 2621440 | tf_op jit(solution)/shard_map/all_to_all | solution.py:35
  16.7 16.5 %all-to-all-done = bf16[8,256,320]{1,2,0:T(8,128)(2,1)S(1)} async-done(((bf16[8,256,320]{1,2,0:T(8,128)(2,1)}), bf16[8,256,320]{1,2,0:T(8,128)(2,1)S(1)}, u32[]{:S(2)}, u32[]{:S(2)}) %all-to-all-start) | async-done | bytes 1310752 | tf_op jit(solution)/shard_map/all_to_all | solution.py:35
  35.7 2.8 %collective-permute-start = (bf16[256,256]{0,1:T(8,128)(2,1)S(1)}, bf16[256,256]{0,1:T(8,128)(2,1)S(1)}, u32[]{:S(2)}, u32[]{:S(2)}) collective-permute-start(bf16[256,256]{0,1:T(8,128)(2,1)S(1)} %convolution_convert_fusion), channel_id=1, source_target_pairs={{0,64},{64,0},{128,192},{192,128},{1,65},{65,1},{129,193},{193,129... | collective-permute-start | bytes 393224 | tf_op jit(solution)/shard_map/ppermute | solution.py:17
  38.5 4.2 %collective-permute-done = bf16[256,256]{0,1:T(8,128)(2,1)S(1)} collective-permute-done((bf16[256,256]{0,1:T(8,128)(2,1)S(1)}, bf16[256,256]{0,1:T(8,128)(2,1)S(1)}, u32[]{:S(2)}, u32[]{:S(2)}) %collective-permute-start) | collective-permute-done | bytes 131104 | tf_op jit(solution)/shard_map/ppermute | solution.py:17
  44.2 6.1 %collective-permute-start.1 = (bf16[1,2,256,256]{2,3,1,0:T(8,128)(2,1)S(1)}, bf16[1,2,256,256]{2,3,1,0:T(8,128)(2,1)S(1)}, u32[]{:S(2)}, u32[]{:S(2)}) collective-permute-start(bf16[1,2,256,256]{2,3,1,0:T(8,128)(2,1)S(1)} %get-tuple-element.24), channel_id=1, source_target_pairs={{0,2},{1,3},{2,4},{3,5},{4,6},{5,7},{6,8},{7,9},{8,10},{9,11},{10,... | collective-permute-start | bytes 786440 | tf_op jit(solution)/shard_map/ppermute | solution.py:23
  50.3 15.3 %collective-permute-done.1 = bf16[1,2,256,256]{2,3,1,0:T(8,128)(2,1)S(1)} collective-permute-done((bf16[1,2,256,256]{2,3,1,0:T(8,128)(2,1)S(1)}, bf16[1,2,256,256]{2,3,1,0:T(8,128)(2,1)S(1)}, u32[]{:S(2)}, u32[]{:S(2)}) %collective-permute-start.1) | collective-permute-done | bytes 262176 | tf_op jit(solution)/shard_map/ppermute | solution.py:23
  65.7 6.0 %collective-permute-start.2 = (bf16[2,2,256,256]{2,3,1,0:T(8,128)(2,1)S(1)}, bf16[2,2,256,256]{2,3,1,0:T(8,128)(2,1)S(1)}, u32[]{:S(2)}, u32[]{:S(2)}) collective-permute-start(bf16[2,2,256,256]{2,3,1,0:T(8,128)(2,1)S(1)} %pad_maximum_fusion.1), channel_id=1, source_target_pairs={{0,4},{1,5},{2,6},{3,7},{4,8},{5,9},{6,10},{7,11},{8,12},{9,13},{1... | collective-permute-start | bytes 1572872 | tf_op jit(solution)/shard_map/ppermute | solution.py:23
  71.7 21.7 %collective-permute-done.2 = bf16[2,2,256,256]{2,3,1,0:T(8,128)(2,1)S(1)} collective-permute-done((bf16[2,2,256,256]{2,3,1,0:T(8,128)(2,1)S(1)}, bf16[2,2,256,256]{2,3,1,0:T(8,128)(2,1)S(1)}, u32[]{:S(2)}, u32[]{:S(2)}) %collective-permute-start.2) | collective-permute-done | bytes 524320 | tf_op jit(solution)/shard_map/ppermute | solution.py:23
  93.5 2.5 collective-permute-start.3
  100.1 33.2 %collective-permute-done.3 = bf16[4,2,256,256]{2,3,1,0:T(8,128)(2,1)S(1)} collective-permute-done((bf16[4,2,256,256]{2,3,1,0:T(8,128)(2,1)S(1)}, bf16[4,2,256,256]{2,3,1,0:T(8,128)(2,1)S(1)}, u32[]{:S(2)}, u32[]{:S(2)}) %collective-permute-start.3) | collective-permute-done | bytes 1048608 | tf_op jit(solution)/shard_map/ppermute | solution.py:23
  134.9 4.8 %collective-permute-done.4 = bf16[2,256,256]{1,2,0:T(8,128)(2,1)S(1)} collective-permute-done((bf16[2,256,256]{1,2,0:T(8,128)(2,1)S(1)}, bf16[2,256,256]{1,2,0:T(8,128)(2,1)S(1)}, u32[]{:S(2)}, u32[]{:S(2)}) %collective-permute-start.4) | collective-permute-done | bytes 262176 | tf_op jit(solution)/shard_map/ppermute | solution.py:23
  144.0 39.1 %all-to-all-start.2 = ((bf16[256,8,320]{0,2,1:T(8,128)(2,1)}), bf16[256,8,320]{0,2,1:T(8,128)(2,1)}, u32[]{:S(2)}, u32[]{:S(2)}) async-start(bf16[256,8,320]{0,2,1:T(8,128)(2,1)} %bitcast.12), calls=%async_computation.2 | async-start | bytes 2621440 | tf_op jit(solution)/shard_map/all_to_all | solution.py:95
  185.9 3.2 %dynamic-slice_dynamic-update-slice_fusion = bf16[17,2,256,256]{2,3,1,0:T(8,128)(2,1)} fusion(bf16[17,2,256,256]{2,3,1,0:T(8,128)(2,1)} %get-tuple-element.18, bf16[9,2,256,256]{2,3,1,0:T(8,128)(2,1)} %collective-permute-done.5, s32[]{:T(128)S(6)} %select_n.64), kind=kLoop, calls=%fused_computation.11 | loop fusion | bytes 4194308 | tf_op jit(solution)/shard_map/concatenate | solution.py:132
  189.0 4.1 %fusion.53 = (bf16[17,1,256,256]{2,3,1,0:T(8,128)(2,1)}, bf16[17,1,256,256]{2,3,1,0:T(8,128)(2,1)S(1)}) fusion(bf16[17,2,256,256]{2,3,1,0:T(8,128)(2,1)} %dynamic-slice_dynamic-update-slice_fusion), kind=kLoop, calls=%fused_computation.106 | loop fusion | bytes 8912896 | tf_op jit(solution)/shard_map/slice | solution.py:133
  193.2 4.2 %copy.27 = bf16[17,1,256,256]{3,2,0,1:T(8,128)(2,1)} copy(bf16[17,1,256,256]{2,3,1,0:T(8,128)(2,1)} %get-tuple-element.9) | data formatting | bytes 4456448 | tf_op jit(solution)/shard_map/slice | solution.py:133
  197.3 2.5 copy.28
  199.8 3.4 %fusion.57 = (f32[256]{0:T(256)S(1)}, f32[256,4352]{1,0:T(8,128)S(1)}) fusion(bf16[4352,256]{1,0:T(8,128)(2,1)} %bitcast.63, bf16[256,128]{0,1:T(8,128)(2,1)} %get-tuple-element.16, bf16[256,128]{0,1:T(8,128)(2,1)} %get-tuple-element.15, s32[256]{0:T(256)S(1)} %iota_add_fusion.1, s32[4352]{0:T(1024)} %copy-done.10, s32[256]{0:T(256)S(1)} %convert_reduce_fusion.1, ...), kind=kOutput, calls=%fused_computation.110 | convolution fusion | flops 577371904 | bytes 6853632 | tf_op jit(solution)/shard_map/dot_general | solution.py:143
  206.9 5.7 %all-to-all-start.1 = ((bf16[8,256,256]{2,1,0:T(8,128)(2,1)}), bf16[8,256,256]{2,1,0:T(8,128)(2,1)S(1)}, u32[]{:S(2)}, u32[]{:S(2)}) async-start(bf16[8,256,256]{2,1,0:T(8,128)(2,1)} %broadcast_in_dim.43), calls=%async_computation.1 | async-start | bytes 2097152 | tf_op jit(solution)/shard_map/all_to_all | solution.py:35
  213.3 14.1 %all-to-all-done.1 = bf16[8,256,256]{2,1,0:T(8,128)(2,1)S(1)} async-done(((bf16[8,256,256]{2,1,0:T(8,128)(2,1)}), bf16[8,256,256]{2,1,0:T(8,128)(2,1)S(1)}, u32[]{:S(2)}, u32[]{:S(2)}) %all-to-all-start.1) | async-done | bytes 1048608 | tf_op jit(solution)/shard_map/all_to_all | solution.py:35
  230.0 3.6 %all-to-all-start.3 = ((f32[8,4,256]{2,1,0:T(4,128)}), f32[8,4,256]{2,1,0:T(4,128)S(1)}, u32[]{:S(2)}, u32[]{:S(2)}) async-start(f32[8,4,256]{2,1,0:T(4,128)} %broadcast_in_dim.44), calls=%async_computation.3 | async-start | bytes 65536 | tf_op jit(solution)/shard_map/all_to_all | solution.py:35
  234.4 5.5 %all-to-all-done.3 = f32[8,4,256]{2,1,0:T(4,128)S(1)} async-done(((f32[8,4,256]{2,1,0:T(4,128)}), f32[8,4,256]{2,1,0:T(4,128)S(1)}, u32[]{:S(2)}, u32[]{:S(2)}) %all-to-all-start.3) | async-done | bytes 32800 | tf_op jit(solution)/shard_map/all_to_all | solution.py:35
  241.2 3.6 %all-to-all-start.4 = ((bf16[8,256,320]{1,2,0:T(8,128)(2,1)}), bf16[8,256,320]{1,2,0:T(8,128)(2,1)S(1)}, u32[]{:S(2)}, u32[]{:S(2)}) async-start(bf16[8,256,320]{1,2,0:T(8,128)(2,1)} %broadcast_in_dim.45), calls=%async_computation.4 | async-start | bytes 2621440 | tf_op jit(solution)/shard_map/all_to_all | solution.py:35
  245.6 15.8 %all-to-all-done.4 = bf16[8,256,320]{1,2,0:T(8,128)(2,1)S(1)} async-done(((bf16[8,256,320]{1,2,0:T(8,128)(2,1)}), bf16[8,256,320]{1,2,0:T(8,128)(2,1)S(1)}, u32[]{:S(2)}, u32[]{:S(2)}) %all-to-all-start.4) | async-done | bytes 1310752 | tf_op jit(solution)/shard_map/all_to_all | solution.py:35
  261.4 4.8 %fusion.58 = f32[256,1280]{1,0:T(8,128)S(1)} fusion(bf16[256,2560]{0,1:T(8,128)(2,1)S(1)} %bitcast.61, bf16[2560,1280]{1,0:T(8,128)(2,1)} %all-gather.2.cloned.1.call-done), kind=kOutput, calls=%fused_computation.111 | convolution fusion | flops 1677721600 | bytes 9175040 | tf_op jit(solution)/shard_map/dot_general | solution.py:186
  (103 shorter events, 30.8 us)
Async XLA Ops:
  7.2 176.7 %copy-start = (bf16[2560,256]{1,0:T(8,128)(2,1)S(1)}, bf16[2560,256]{1,0:T(8,128)(2,1)}, u32[]{:S(2)}) copy-start(bf16[2560,256]{1,0:T(8,128)(2,1)} %param.14) | copy-start | bytes 3932164
  7.2 8.5 %copy-start.11 = (bf16[40,2,640]{2,1,0:T(2,128)(2,1)S(1)}, bf16[40,2,640]{2,1,0:T(2,128)(2,1)}, u32[]{:S(2)}) copy-start(bf16[40,2,640]{2,1,0:T(2,128)(2,1)} %param.17) | copy-start | bytes 307204
  7.2 9.2 %copy-start.16 = (s32[8]{0:T(128)S(1)}, s32[8]{0:T(128)}, u32[]{:S(2)}) copy-start(s32[8]{0:T(128)} %param.23) | copy-start | bytes 100
  9.4 24.2 %copy-start.12 = (f32[2560]{0:T(1024)S(1)}, f32[2560]{0:T(1024)}, u32[]{:S(2)}) copy-start(f32[2560]{0:T(1024)} %param.18) | copy-start | bytes 30724
  9.4 23.8 %all-to-all-start = ((bf16[8,256,320]{1,2,0:T(8,128)(2,1)}), bf16[8,256,320]{1,2,0:T(8,128)(2,1)S(1)}, u32[]{:S(2)}, u32[]{:S(2)}) async-start(bf16[8,256,320]{1,2,0:T(8,128)(2,1)} %broadcast_in_dim.36), calls=%async_computation | async-start | bytes 2621440 | tf_op jit(solution)/shard_map/all_to_all | solution.py:35
  15.6 245.8 %all-gather.2.cloned.1.call-start = ((), (), s32[]{:S(2)}) async-start(), calls=%async_computation.5 | async-start | bytes 6656000 | tf_op jit(solution)/shard_map/all_gather | solution.py:183
  35.1 7.8 %copy-start.13 = (f32[256]{0:T(256)S(1)}, f32[256]{0:T(256)}, u32[]{:S(2)}) copy-start(f32[256]{0:T(256)} %param.22) | copy-start | bytes 3076
  35.7 57.8 %copy-start.7 = (bf16[256,256]{0,1:T(8,128)(2,1)}, bf16[256,256]{0,1:T(8,128)(2,1)S(1)}, u32[]{:S(2)}) copy-start(bf16[256,256]{0,1:T(8,128)(2,1)S(1)} %convolution_convert_fusion) | copy-start | bytes 393220
  35.7 7.0 %collective-permute-start = (bf16[256,256]{0,1:T(8,128)(2,1)S(1)}, bf16[256,256]{0,1:T(8,128)(2,1)S(1)}, u32[]{:S(2)}, u32[]{:S(2)}) collective-permute-start(bf16[256,256]{0,1:T(8,128)(2,1)S(1)} %convolution_convert_fusion), channel_id=1, source_target_pairs={{0,64},{64,0},{128,192},{192,128},{1,65},{65,1},{129,193},{193,129... | collective-permute-start | bytes 393224 | tf_op jit(solution)/shard_map/ppermute | solution.py:17
  44.2 21.4 %collective-permute-start.1 = (bf16[1,2,256,256]{2,3,1,0:T(8,128)(2,1)S(1)}, bf16[1,2,256,256]{2,3,1,0:T(8,128)(2,1)S(1)}, u32[]{:S(2)}, u32[]{:S(2)}) collective-permute-start(bf16[1,2,256,256]{2,3,1,0:T(8,128)(2,1)S(1)} %get-tuple-element.24), channel_id=1, source_target_pairs={{0,2},{1,3},{2,4},{3,5},{4,6},{5,7},{6,8},{7,9},{8,10},{9,11},{10,... | collective-permute-start | bytes 786440 | tf_op jit(solution)/shard_map/ppermute | solution.py:23
  65.7 27.8 %collective-permute-start.2 = (bf16[2,2,256,256]{2,3,1,0:T(8,128)(2,1)S(1)}, bf16[2,2,256,256]{2,3,1,0:T(8,128)(2,1)S(1)}, u32[]{:S(2)}, u32[]{:S(2)}) collective-permute-start(bf16[2,2,256,256]{2,3,1,0:T(8,128)(2,1)S(1)} %pad_maximum_fusion.1), channel_id=1, source_target_pairs={{0,4},{1,5},{2,6},{3,7},{4,8},{5,9},{6,10},{7,11},{8,12},{9,13},{1... | collective-permute-start | bytes 1572872 | tf_op jit(solution)/shard_map/ppermute | solution.py:23
  93.5 39.7 %collective-permute-start.3 = (bf16[4,2,256,256]{2,3,1,0:T(8,128)(2,1)S(1)}, bf16[4,2,256,256]{2,3,1,0:T(8,128)(2,1)S(1)}, u32[]{:S(2)}, u32[]{:S(2)}) collective-permute-start(bf16[4,2,256,256]{2,3,1,0:T(8,128)(2,1)S(1)} %pad_maximum_fusion), channel_id=1, source_target_pairs={{0,8},{1,9},{2,10},{3,11},{4,12},{5,13},{6,14},{7,15},{8,16},{9,17... | collective-permute-start | bytes 3145736 | tf_op jit(solution)/shard_map/ppermute | solution.py:23
  96.0 43.6 %collective-permute-start.4 = (bf16[2,256,256]{1,2,0:T(8,128)(2,1)S(1)}, bf16[2,256,256]{1,2,0:T(8,128)(2,1)S(1)}, u32[]{:S(2)}, u32[]{:S(2)}) collective-permute-start(bf16[2,256,256]{1,2,0:T(8,128)(2,1)S(1)} %get-tuple-element.23), channel_id=1, source_target_pairs={{0,16},{1,17},{2,18},{3,19},{4,20},{5,21},{6,22},{7,23},{8,24},{9,... | collective-permute-start | bytes 786440 | tf_op jit(solution)/shard_map/ppermute | solution.py:23
  100.1 42.5 %copy-start.2 = (bf16[256,2560]{1,0:T(8,128)(2,1)S(1)}, bf16[256,2560]{1,0:T(8,128)(2,1)}, u32[]{:S(2)}) copy-start(bf16[256,2560]{1,0:T(8,128)(2,1)} %param.16) | copy-start | bytes 3932164
  140.5 42.6 %copy-start.18 = (s32[17]{0:T(128)S(1)}, s32[17]{0:T(128)}, u32[]{:S(2)}) copy-start(s32[17]{0:T(128)} %constant.99) | copy-start | bytes 208
  140.5 45.4 %collective-permute-start.5 = (bf16[9,2,256,256]{2,3,1,0:T(8,128)(2,1)}, bf16[9,2,256,256]{2,3,1,0:T(8,128)(2,1)}, u32[]{:S(2)}, u32[]{:S(2)}) collective-permute-start(bf16[9,2,256,256]{2,3,1,0:T(8,128)(2,1)} %get-tuple-element.17), channel_id=1, source_target_pairs={{0,1},{1,0},{2,3},{3,2},{4,5},{5,4},{6,7},{7,6},{8,9},{9,8},{10,11... | collective-permute-start | bytes 7077896 | tf_op jit(solution)/shard_map/ppermute | solution.py:17
  144.0 39.9 %copy-start.4 = (bf16[256,2560]{0,1:T(8,128)(2,1)S(1)}, bf16[256,2560]{0,1:T(8,128)(2,1)}, u32[]{:S(2)}) copy-start(bf16[256,2560]{0,1:T(8,128)(2,1)} %copy-done.3) | copy-start | bytes 3932164
  144.0 40.5 %copy-start.14 = (f32[256]{0:T(256)S(1)}, f32[256]{0:T(256)}, u32[]{:S(2)}) copy-start(f32[256]{0:T(256)} %param.21) | copy-start | bytes 3076
  144.0 61.8 %all-to-all-start.2 = ((bf16[256,8,320]{0,2,1:T(8,128)(2,1)}), bf16[256,8,320]{0,2,1:T(8,128)(2,1)}, u32[]{:S(2)}, u32[]{:S(2)}) async-start(bf16[256,8,320]{0,2,1:T(8,128)(2,1)} %bitcast.12), calls=%async_computation.2 | async-start | bytes 2621440 | tf_op jit(solution)/shard_map/all_to_all | solution.py:95
  205.8 21.7 %copy-start.5 = (bf16[256,320]{0,1:T(8,128)(2,1)S(1)}, bf16[256,320]{0,1:T(8,128)(2,1)}, u32[]{:S(2)}) copy-start(bf16[256,320]{0,1:T(8,128)(2,1)} %param.13) | copy-start | bytes 491524
  206.9 20.6 %all-to-all-start.1 = ((bf16[8,256,256]{2,1,0:T(8,128)(2,1)}), bf16[8,256,256]{2,1,0:T(8,128)(2,1)S(1)}, u32[]{:S(2)}, u32[]{:S(2)}) async-start(bf16[8,256,256]{2,1,0:T(8,128)(2,1)} %broadcast_in_dim.43), calls=%async_computation.1 | async-start | bytes 2097152 | tf_op jit(solution)/shard_map/all_to_all | solution.py:35
  230.0 9.9 %all-to-all-start.3 = ((f32[8,4,256]{2,1,0:T(4,128)}), f32[8,4,256]{2,1,0:T(4,128)S(1)}, u32[]{:S(2)}, u32[]{:S(2)}) async-start(f32[8,4,256]{2,1,0:T(4,128)} %broadcast_in_dim.44), calls=%async_computation.3 | async-start | bytes 65536 | tf_op jit(solution)/shard_map/all_to_all | solution.py:35
  241.2 20.2 %all-to-all-start.4 = ((bf16[8,256,320]{1,2,0:T(8,128)(2,1)}), bf16[8,256,320]{1,2,0:T(8,128)(2,1)S(1)}, u32[]{:S(2)}, u32[]{:S(2)}) async-start(bf16[8,256,320]{1,2,0:T(8,128)(2,1)} %broadcast_in_dim.45), calls=%async_computation.4 | async-start | bytes 2621440 | tf_op jit(solution)/shard_map/all_to_all | solution.py:35
  245.6 20.5 %copy-start.6 = (bf16[2,128,256]{2,1,0:T(8,128)(2,1)}, bf16[2,128,256]{2,1,0:T(8,128)(2,1)S(1)}, u32[]{:S(2)}) copy-start(bf16[2,128,256]{2,1,0:T(8,128)(2,1)S(1)} %scatter_fusion) | copy-start | bytes 393220
  (7 other events, 22.0 us)
Sparse Core Ops, SparseCore 0:
  20.3 127.1 all-gather.1
where the time goes:
time: 275 us; the launch traced here: 274 us
  waiting for transfers between devices  131 us (48%)
  starting transfers between devices  79 us (29%)
  local copies, waits for them, and re-layouts  29.6 us (11%)
  between operations  14.5 us (5%)
  matrix products  12.2 us (4%)
  other arithmetic  7.65 us (3%)
    ppermute x4, waiting for transfers between devices, shifted(): return lax.ppermute(block, axis, route)  74.9 us
    all_to_all x4, waiting for transfers between devices, group_parts(): return lax.all_to_all(spread, GROUP, 0, 0, tiled=True)  51.9 us
    all_to_all x1, starting transfers between devices, local(): out_columns = lax.all_to_all(w_out, GROUP, 1, 0, tiled=True)  39.1 us
    all_to_all x4, starting transfers between devices, group_parts(): return lax.all_to_all(spread, GROUP, 0, 0, tiled=True)  19.1 us
    ppermute x4, starting transfers between devices, shifted(): return lax.ppermute(block, axis, route)  15.9 us
    slice x2, local copies, waits for them, and re-layouts, local(): all_keys = window_stack[:, 0].reshape(-1, head_width)  8.29 us
    unnamed x43, local copies, waits for them, and re-layouts  7.61 us
  transfers between devices with their start and end apart: 12, of which 9 were waited for; matrix products, arithmetic and copies ran while one was open for 14% of the time, Pallas kernels for 0%

commit v1 on v0

--- a/solution.py
+++ b/solution.py
@@ -128,30 +128,40 @@
     series = jnp.concatenate([series, shifted(key_block, "seq", 2 * half_span)[None]], axis=0)
     partner = swapped(series, "seq", 0)
     parity = lax.axis_index("seq") % 2
-    odd = lax.dynamic_slice_in_dim(partner, 1 - parity, half_span, axis=0)
-    window_stack = jnp.concatenate([series, odd], axis=0)
-    all_keys = window_stack[:, 0].reshape(-1, head_width)
-    all_values = window_stack[:, 1].reshape(-1, head_width)
-    distances = list(range(0, 2 * half_span + 1, 2)) + list(range(1, 2 * half_span, 2))
-    offsets = (jnp.array(distances, dtype=jnp.int32) * row_count)[:, None]
-    key_index = (first_row - offsets + jnp.arange(row_count, dtype=jnp.int32)[None, :]).reshape(-1)
-    key_segment = jnp.sum((prompt_ends[None, :] <= key_index[:, None]).astype(jnp.int32), axis=1)
-    key_segment = jnp.where(key_index >= 0, key_segment, -1)
-    allowed = (key_segment[None, :] == query_segment[:, None]) & (
-        key_index[None, :] <= query_index[:, None]
-    )
-    scores = lax.dot_general(
-        queries, all_keys, (((1,), (1,)), ((), ())), preferred_element_type=jnp.float32
-    ) * head_width ** (-0.5)
-    scores = jnp.where(allowed, scores, -jnp.inf)
-    row_max = jnp.max(scores, axis=1, keepdims=True)
-    exponent_terms = jnp.exp(scores - row_max)
-    weights_low = (exponent_terms / jnp.sum(exponent_terms, axis=1, keepdims=True)).astype(
-        jnp.bfloat16
-    )
-    attention_out = jnp.dot(weights_low, all_values, preferred_element_type=jnp.float32).astype(
-        jnp.bfloat16
-    )
+    lanes = jnp.arange(row_count, dtype=jnp.int32)[None, :]
+    own_offsets = jnp.arange(series.shape[0], dtype=jnp.int32)[:, None] * (2 * row_count)
+    partner_offsets = own_offsets + (2 * parity - 1) * row_count
+    score_scale = head_width ** (-0.5)
+
+    def part_scores(stack, offsets):
+        key_index = (first_row - offsets + lanes).reshape(-1)
+        key_segment = jnp.sum((prompt_ends[None, :] <= key_index[:, None]).astype(jnp.int32), axis=1)
+        key_segment = jnp.where(key_index >= 0, key_segment, -1)
+        allowed = (key_segment[None, :] == query_segment[:, None]) & (
+            key_index[None, :] <= query_index[:, None]
+        )
+        keys = stack[:, 0].reshape(-1, head_width)
+        scores = lax.dot_general(
+            queries, keys, (((1,), (1,)), ((), ())), preferred_element_type=jnp.float32
+        ) * score_scale
+        return jnp.where(allowed, scores, -jnp.inf)
+
+    own_scores = part_scores(series, own_offsets)
+    partner_scores = part_scores(partner, partner_offsets)
+    row_max = jnp.maximum(
+        jnp.max(own_scores, axis=1, keepdims=True), jnp.max(partner_scores, axis=1, keepdims=True)
+    )
+    own_terms = jnp.exp(own_scores - row_max)
+    partner_terms = jnp.exp(partner_scores - row_max)
+    total = jnp.sum(own_terms, axis=1, keepdims=True) + jnp.sum(partner_terms, axis=1, keepdims=True)
+    own_probs = (own_terms / total).astype(jnp.bfloat16)
+    partner_probs = (partner_terms / total).astype(jnp.bfloat16)
+    attention_out = (
+        jnp.dot(own_probs, series[:, 1].reshape(-1, head_width), preferred_element_type=jnp.float32)
+        + jnp.dot(
+            partner_probs, partner[:, 1].reshape(-1, head_width), preferred_element_type=jnp.float32
+        )
+    ).astype(jnp.bfloat16)
     all_heads = group_gather(attention_out)
     attended = jnp.dot(all_heads, out_columns, preferred_element_type=jnp.float32)
     width = attended.shape[1]

time: 275 us -> 274 us (level)
  waiting for transfers between devices: 131 us -> 100 us
  starting transfers between devices: 79 us -> 103 us
  matrix products: 12.2 us -> 15.1 us
    ppermute x4, waiting for transfers between devices: 74.9 us -> 43.9 us  [shifted(): return lax.ppermute(block, axis, route)]
    all_to_all x4, starting transfers between devices: 19.1 us -> 38.2 us  [group_parts(): return lax.all_to_all(spread, GROUP, 0, 0, tiled=True)]
    all_to_all x1, starting transfers between devices: 39.1 us -> 43.5 us  [local(): out_columns = lax.all_to_all(w_out, GROUP, 1, 0, tiled=True)]
    concatenate x1 -> x0, local copies, waits for them, and re-layouts: 3.15 us -> none  [local(): window_stack = jnp.concatenate([series, odd], axis=0)]
    dot_general x2 -> x4, matrix products: 4.34 us -> 7.17 us  [the longest x2 5.97 us: part_scores(): lax.dot_general(queries, keys, (((1,), (1,)), ((), ())), preferred_elemen...]
    slice x3 -> x6, local copies, waits for them, and re-layouts: 10.8 us -> 13.6 us  [the longest x3 7.67 us: part_scores(): keys = stack[:, 0].reshape(-1, head_width)]
    unnamed x43 -> x63, local copies, waits for them, and re-layouts: 7.61 us -> 8.74 us
  transfers between devices with their start and end apart: 12 -> 12, of which waited for: 9 -> 8; matrix products, arithmetic and copies ran while one was open for 14% -> 16% of each run, Pallas kernels for 0% -> 0%
where the time goes in v1:
time: 274 us; the launch traced here: 273 us
  starting transfers between devices  103 us (38%)
  waiting for transfers between devices  100 us (36%)
  local copies, waits for them, and re-layouts  30.3 us (11%)
  matrix products  15.1 us (6%)
  between operations  14.6 us (5%)
  other arithmetic  10 us (4%)
    all_to_all x4, waiting for transfers between devices, group_parts(): return lax.all_to_all(spread, GROUP, 0, 0, tiled=True)  52 us
    ppermute x4, waiting for transfers between devices, shifted(): return lax.ppermute(block, axis, route)  43.9 us
    all_to_all x1, starting transfers between devices, local(): out_columns = lax.all_to_all(w_out, GROUP, 1, 0, tiled=True)  43.5 us
    all_to_all x4, starting transfers between devices, group_parts(): return lax.all_to_all(spread, GROUP, 0, 0, tiled=True)  38.2 us
    ppermute x4, starting transfers between devices, shifted(): return lax.ppermute(block, axis, route)  16.6 us
    unnamed x63, local copies, waits for them, and re-layouts  8.74 us
    slice x3, local copies, waits for them, and re-layouts, part_scores(): keys = stack[:, 0].reshape(-1, head_width)  7.67 us
    dot_general x2, matrix products, part_scores(): lax.dot_general(queries, keys, (((1,), (1,)), ((), ())), preferred_elemen...  5.97 us
  transfers between devices with their start and end apart: 12, of which 8 were waited for; matrix products, arithmetic and copies ran while one was open for 16% of the time, Pallas kernels for 0%

profile of v1, /device:TPU:48, one launch (start us, length us, event | category | flops | bytes accessed | tf_op | source)
XLA Modules:
  0.0 273.1 jit_solution(10862794532566245058)
XLA Ops:
  9.4 6.2 %all-to-all-start = ((bf16[8,256,320]{1,2,0:T(8,128)(2,1)}), bf16[8,256,320]{1,2,0:T(8,128)(2,1)S(1)}, u32[]{:S(2)}, u32[]{:S(2)}) async-start(bf16[8,256,320]{1,2,0:T(8,128)(2,1)} %broadcast_in_dim.39), calls=%async_computation | async-start | bytes 2621440 | tf_op jit(solution)/shard_map/all_to_all | solution.py:35
  17.2 16.0 %all-to-all-done = bf16[8,256,320]{1,2,0:T(8,128)(2,1)S(1)} async-done(((bf16[8,256,320]{1,2,0:T(8,128)(2,1)}), bf16[8,256,320]{1,2,0:T(8,128)(2,1)S(1)}, u32[]{:S(2)}, u32[]{:S(2)}) %all-to-all-start) | async-done | bytes 1310752 | tf_op jit(solution)/shard_map/all_to_all | solution.py:35
  35.8 2.8 %collective-permute-start = (bf16[256,256]{0,1:T(8,128)(2,1)S(1)}, bf16[256,256]{0,1:T(8,128)(2,1)S(1)}, u32[]{:S(2)}, u32[]{:S(2)}) collective-permute-start(bf16[256,256]{0,1:T(8,128)(2,1)S(1)} %convolution_convert_fusion), channel_id=1, source_target_pairs={{0,64},{64,0},{128,192},{192,128},{1,65},{65,1},{129,193},{193,129... | collective-permute-start | bytes 393224 | tf_op jit(solution)/shard_map/ppermute | solution.py:17
  38.6 4.2 %collective-permute-done = bf16[256,256]{0,1:T(8,128)(2,1)S(1)} collective-permute-done((bf16[256,256]{0,1:T(8,128)(2,1)S(1)}, bf16[256,256]{0,1:T(8,128)(2,1)S(1)}, u32[]{:S(2)}, u32[]{:S(2)}) %collective-permute-start) | collective-permute-done | bytes 131104 | tf_op jit(solution)/shard_map/ppermute | solution.py:17
  45.0 6.1 %collective-permute-start.1 = (bf16[1,2,256,256]{2,3,1,0:T(8,128)(2,1)S(1)}, bf16[1,2,256,256]{2,3,1,0:T(8,128)(2,1)S(1)}, u32[]{:S(2)}, u32[]{:S(2)}) collective-permute-start(bf16[1,2,256,256]{2,3,1,0:T(8,128)(2,1)S(1)} %get-tuple-element.20), channel_id=1, source_target_pairs={{0,2},{1,3},{2,4},{3,5},{4,6},{5,7},{6,8},{7,9},{8,10},{9,11},{10,... | collective-permute-start | bytes 786440 | tf_op jit(solution)/shard_map/ppermute | solution.py:23
  51.1 14.8 %collective-permute-done.1 = bf16[1,2,256,256]{2,3,1,0:T(8,128)(2,1)S(1)} collective-permute-done((bf16[1,2,256,256]{2,3,1,0:T(8,128)(2,1)S(1)}, bf16[1,2,256,256]{2,3,1,0:T(8,128)(2,1)S(1)}, u32[]{:S(2)}, u32[]{:S(2)}) %collective-permute-start.1) | collective-permute-done | bytes 262176 | tf_op jit(solution)/shard_map/ppermute | solution.py:23
  66.0 6.1 %collective-permute-start.2 = (bf16[2,2,256,256]{2,3,1,0:T(8,128)(2,1)S(1)}, bf16[2,2,256,256]{2,3,1,0:T(8,128)(2,1)S(1)}, u32[]{:S(2)}, u32[]{:S(2)}) collective-permute-start(bf16[2,2,256,256]{2,3,1,0:T(8,128)(2,1)S(1)} %pad_maximum_fusion.1), channel_id=1, source_target_pairs={{0,4},{1,5},{2,6},{3,7},{4,8},{5,9},{6,10},{7,11},{8,12},{9,13},{1... | collective-permute-start | bytes 1572872 | tf_op jit(solution)/shard_map/ppermute | solution.py:23
  72.1 20.1 %collective-permute-done.2 = bf16[2,2,256,256]{2,3,1,0:T(8,128)(2,1)S(1)} collective-permute-done((bf16[2,2,256,256]{2,3,1,0:T(8,128)(2,1)S(1)}, bf16[2,2,256,256]{2,3,1,0:T(8,128)(2,1)S(1)}, u32[]{:S(2)}, u32[]{:S(2)}) %collective-permute-start.2) | collective-permute-done | bytes 524320 | tf_op jit(solution)/shard_map/ppermute | solution.py:23
  93.2 3.0 %collective-permute-start.3 = (bf16[4,2,256,256]{2,3,1,0:T(8,128)(2,1)}, bf16[4,2,256,256]{2,3,1,0:T(8,128)(2,1)}, u32[]{:S(2)}, u32[]{:S(2)}) collective-permute-start(bf16[4,2,256,256]{2,3,1,0:T(8,128)(2,1)} %pad_maximum_fusion), channel_id=1, source_target_pairs={{0,8},{1,9},{2,10},{3,11},{4,12},{5,13},{6,14},{7,15},{8,16},{9,17... | collective-permute-start | bytes 3145736 | tf_op jit(solution)/shard_map/ppermute | solution.py:23
  97.7 43.5 %all-to-all-start.2 = ((bf16[256,8,320]{0,2,1:T(8,128)(2,1)}), bf16[256,8,320]{0,2,1:T(8,128)(2,1)}, u32[]{:S(2)}, u32[]{:S(2)}) async-start(bf16[256,8,320]{0,2,1:T(8,128)(2,1)} %bitcast.14), calls=%async_computation.2 | async-start | bytes 2621440 | tf_op jit(solution)/shard_map/all_to_all | solution.py:95
  148.7 9.0 %collective-permute-done.4 = bf16[2,256,256]{1,2,0:T(8,128)(2,1)S(1)} collective-permute-done((bf16[2,256,256]{1,2,0:T(8,128)(2,1)}, bf16[2,256,256]{1,2,0:T(8,128)(2,1)S(1)}, u32[]{:S(2)}, u32[]{:S(2)}) %collective-permute-start.4) | collective-permute-done | bytes 262176 | tf_op jit(solution)/shard_map/ppermute | solution.py:23
  162.6 2.8 %fusion.57 = (bf16[9,1,256,256]{2,3,1,0:T(8,128)(2,1)}, bf16[9,1,256,256]{2,3,1,0:T(8,128)(2,1)S(1)}) fusion(bf16[9,2,256,256]{2,3,1,0:T(8,128)(2,1)} %bitcast_dynamic-update-slice_fusion), kind=kLoop, calls=%fused_computation.112 | loop fusion | bytes 4718592 | tf_op jit(solution)/shard_map/slice | solution.py:143
  165.4 2.4 copy.30
  169.4 3.6 %fusion.61 = (f32[256]{0:T(256)S(1)}, f32[256,2304]{1,0:T(8,128)}) fusion(bf16[2304,256]{1,0:T(8,128)(2,1)} %bitcast.67, bf16[256,128]{0,1:T(8,128)(2,1)S(1)} %get-tuple-element.18, bf16[256,128]{0,1:T(8,128)(2,1)S(1)} %get-tuple-element.17, s32[256]{0:T(256)S(1)} %copy-done.25, s32[2304]{0:T(1024)S(1)} %add.186, s32[256]{0:T(256)S(1)} %copy-done.17, ...), kind=kOutput, calls=%fused_computation.116 | convolution fusion | flops 305790720 | bytes 3691520 | tf_op jit(solution)/shard_map/dot_general | solution.py:144
  172.9 2.8 %fusion.56 = (bf16[9,1,256,256]{2,3,1,0:T(8,128)(2,1)S(1)}, bf16[9,1,256,256]{2,3,1,0:T(8,128)(2,1)}) fusion(bf16[9,2,256,256]{2,3,1,0:T(8,128)(2,1)} %collective-permute-done.5), kind=kLoop, calls=%fused_computation.111 | loop fusion | bytes 4718592 | tf_op jit(solution)/shard_map/slice | solution.py:162
  175.8 2.4 copy.31
  179.7 2.4 fusion.62
  186.4 24.7 %all-to-all-start.1 = ((bf16[8,256,256]{2,1,0:T(8,128)(2,1)}), bf16[8,256,256]{2,1,0:T(8,128)(2,1)S(1)}, u32[]{:S(2)}, u32[]{:S(2)}) async-start(bf16[8,256,256]{2,1,0:T(8,128)(2,1)} %broadcast_in_dim.45), calls=%async_computation.1 | async-start | bytes 2097152 | tf_op jit(solution)/shard_map/all_to_all | solution.py:35
  211.8 14.7 %all-to-all-done.1 = bf16[8,256,256]{2,1,0:T(8,128)(2,1)S(1)} async-done(((bf16[8,256,256]{2,1,0:T(8,128)(2,1)}), bf16[8,256,256]{2,1,0:T(8,128)(2,1)S(1)}, u32[]{:S(2)}, u32[]{:S(2)}) %all-to-all-start.1) | async-done | bytes 1048608 | tf_op jit(solution)/shard_map/all_to_all | solution.py:35
  229.0 3.6 %all-to-all-start.3 = ((f32[8,4,256]{2,1,0:T(4,128)}), f32[8,4,256]{2,1,0:T(4,128)S(1)}, u32[]{:S(2)}, u32[]{:S(2)}) async-start(f32[8,4,256]{2,1,0:T(4,128)} %broadcast_in_dim.46), calls=%async_computation.3 | async-start | bytes 65536 | tf_op jit(solution)/shard_map/all_to_all | solution.py:35
  233.5 5.5 %all-to-all-done.3 = f32[8,4,256]{2,1,0:T(4,128)S(1)} async-done(((f32[8,4,256]{2,1,0:T(4,128)}), f32[8,4,256]{2,1,0:T(4,128)S(1)}, u32[]{:S(2)}, u32[]{:S(2)}) %all-to-all-start.3) | async-done | bytes 32800 | tf_op jit(solution)/shard_map/all_to_all | solution.py:35
  240.3 3.6 %all-to-all-start.4 = ((bf16[8,256,320]{1,2,0:T(8,128)(2,1)}), bf16[8,256,320]{1,2,0:T(8,128)(2,1)S(1)}, u32[]{:S(2)}, u32[]{:S(2)}) async-start(bf16[8,256,320]{1,2,0:T(8,128)(2,1)} %broadcast_in_dim.47), calls=%async_computation.4 | async-start | bytes 2621440 | tf_op jit(solution)/shard_map/all_to_all | solution.py:35
  244.7 15.8 %all-to-all-done.4 = bf16[8,256,320]{1,2,0:T(8,128)(2,1)S(1)} async-done(((bf16[8,256,320]{1,2,0:T(8,128)(2,1)}), bf16[8,256,320]{1,2,0:T(8,128)(2,1)S(1)}, u32[]{:S(2)}, u32[]{:S(2)}) %all-to-all-start.4) | async-done | bytes 1310752 | tf_op jit(solution)/shard_map/all_to_all | solution.py:35
  260.5 4.8 %fusion.63 = f32[256,1280]{1,0:T(8,128)S(1)} fusion(bf16[256,2560]{0,1:T(8,128)(2,1)S(1)} %bitcast.63, bf16[2560,1280]{1,0:T(8,128)(2,1)} %all-gather.2.cloned.1.call-done), kind=kOutput, calls=%fused_computation.118 | convolution fusion | flops 1677721600 | bytes 9175040 | tf_op jit(solution)/shard_map/dot_general | solution.py:196
  (132 shorter events, 37.6 us)
Async XLA Ops:
  7.2 154.0 %copy-start = (bf16[2560,256]{1,0:T(8,128)(2,1)S(1)}, bf16[2560,256]{1,0:T(8,128)(2,1)}, u32[]{:S(2)}) copy-start(bf16[2560,256]{1,0:T(8,128)(2,1)} %param.13) | copy-start | bytes 3932164
  9.4 24.2 %copy-start.15 = (f32[2560]{0:T(1024)S(1)}, f32[2560]{0:T(1024)}, u32[]{:S(2)}) copy-start(f32[2560]{0:T(1024)} %param.17) | copy-start | bytes 30724
  9.4 23.8 %all-to-all-start = ((bf16[8,256,320]{1,2,0:T(8,128)(2,1)}), bf16[8,256,320]{1,2,0:T(8,128)(2,1)S(1)}, u32[]{:S(2)}, u32[]{:S(2)}) async-start(bf16[8,256,320]{1,2,0:T(8,128)(2,1)} %broadcast_in_dim.39), calls=%async_computation | async-start | bytes 2621440 | tf_op jit(solution)/shard_map/all_to_all | solution.py:35
  15.6 244.9 %all-gather.2.cloned.1.call-start = ((), (), s32[]{:S(2)}) async-start(), calls=%async_computation.5 | async-start | bytes 6656000 | tf_op jit(solution)/shard_map/all_gather | solution.py:193
  17.1 16.1 %copy-start.16 = (s32[256]{0:T(256)}, s32[256]{0:T(256)S(1)}, u32[]{:S(2)}) copy-start(s32[256]{0:T(256)S(1)} %convert_reduce_fusion.2) | copy-start | bytes 3076
  35.8 7.0 %collective-permute-start = (bf16[256,256]{0,1:T(8,128)(2,1)S(1)}, bf16[256,256]{0,1:T(8,128)(2,1)S(1)}, u32[]{:S(2)}, u32[]{:S(2)}) collective-permute-start(bf16[256,256]{0,1:T(8,128)(2,1)S(1)} %convolution_convert_fusion), channel_id=1, source_target_pairs={{0,64},{64,0},{128,192},{192,128},{1,65},{65,1},{129,193},{193,129... | collective-permute-start | bytes 393224 | tf_op jit(solution)/shard_map/ppermute | solution.py:17
  38.6 54.7 %copy-start.18 = (f32[128]{0:T(128)}, f32[128]{0:T(128)S(1)}, u32[]{:S(2)}) copy-start(f32[128]{0:T(128)S(1)} %negate_power_fusion) | copy-start | bytes 1540
  42.9 53.3 %copy-start.2 = (bf16[256,2560]{1,0:T(8,128)(2,1)S(1)}, bf16[256,2560]{1,0:T(8,128)(2,1)}, u32[]{:S(2)}) copy-start(bf16[256,2560]{1,0:T(8,128)(2,1)} %param.15) | copy-start | bytes 3932164
  44.2 21.7 %copy-start.8 = (bf16[256,128]{0,1:T(8,128)(2,1)}, bf16[256,128]{0,1:T(8,128)(2,1)S(1)}, u32[]{:S(2)}) copy-start(bf16[256,128]{0,1:T(8,128)(2,1)S(1)} %get-tuple-element.11) | copy-start | bytes 196612
  44.2 27.9 %copy-start.9 = (bf16[256,128]{0,1:T(8,128)(2,1)}, bf16[256,128]{0,1:T(8,128)(2,1)S(1)}, u32[]{:S(2)}) copy-start(bf16[256,128]{0,1:T(8,128)(2,1)S(1)} %get-tuple-element.12) | copy-start | bytes 196612
  45.0 20.9 %collective-permute-start.1 = (bf16[1,2,256,256]{2,3,1,0:T(8,128)(2,1)S(1)}, bf16[1,2,256,256]{2,3,1,0:T(8,128)(2,1)S(1)}, u32[]{:S(2)}, u32[]{:S(2)}) collective-permute-start(bf16[1,2,256,256]{2,3,1,0:T(8,128)(2,1)S(1)} %get-tuple-element.20), channel_id=1, source_target_pairs={{0,2},{1,3},{2,4},{3,5},{4,6},{5,7},{6,8},{7,9},{8,10},{9,11},{10,... | collective-permute-start | bytes 786440 | tf_op jit(solution)/shard_map/ppermute | solution.py:23
  66.0 26.2 %collective-permute-start.2 = (bf16[2,2,256,256]{2,3,1,0:T(8,128)(2,1)S(1)}, bf16[2,2,256,256]{2,3,1,0:T(8,128)(2,1)S(1)}, u32[]{:S(2)}, u32[]{:S(2)}) collective-permute-start(bf16[2,2,256,256]{2,3,1,0:T(8,128)(2,1)S(1)} %pad_maximum_fusion.1), channel_id=1, source_target_pairs={{0,4},{1,5},{2,6},{3,7},{4,8},{5,9},{6,10},{7,11},{8,12},{9,13},{1... | collective-permute-start | bytes 1572872 | tf_op jit(solution)/shard_map/ppermute | solution.py:23
  93.2 53.1 %collective-permute-start.3 = (bf16[4,2,256,256]{2,3,1,0:T(8,128)(2,1)}, bf16[4,2,256,256]{2,3,1,0:T(8,128)(2,1)}, u32[]{:S(2)}, u32[]{:S(2)}) collective-permute-start(bf16[4,2,256,256]{2,3,1,0:T(8,128)(2,1)} %pad_maximum_fusion), channel_id=1, source_target_pairs={{0,8},{1,9},{2,10},{3,11},{4,12},{5,13},{6,14},{7,15},{8,16},{9,17... | collective-permute-start | bytes 3145736 | tf_op jit(solution)/shard_map/ppermute | solution.py:23
  97.7 87.6 %all-to-all-start.2 = ((bf16[256,8,320]{0,2,1:T(8,128)(2,1)}), bf16[256,8,320]{0,2,1:T(8,128)(2,1)}, u32[]{:S(2)}, u32[]{:S(2)}) async-start(bf16[256,8,320]{0,2,1:T(8,128)(2,1)} %bitcast.14), calls=%async_computation.2 | async-start | bytes 2621440 | tf_op jit(solution)/shard_map/all_to_all | solution.py:95
  141.8 18.6 %copy-start.21 = (s32[9]{0:T(128)S(1)}, s32[9]{0:T(128)}, u32[]{:S(2)}) copy-start(s32[9]{0:T(128)} %get-tuple-element.40) | copy-start | bytes 112
  141.8 19.4 %copy-start.4 = (bf16[256,2560]{0,1:T(8,128)(2,1)S(1)}, bf16[256,2560]{0,1:T(8,128)(2,1)}, u32[]{:S(2)}) copy-start(bf16[256,2560]{0,1:T(8,128)(2,1)} %copy-done.3) | copy-start | bytes 3932164
  141.8 15.9 %collective-permute-start.4 = (bf16[2,256,256]{1,2,0:T(8,128)(2,1)}, bf16[2,256,256]{1,2,0:T(8,128)(2,1)S(1)}, u32[]{:S(2)}, u32[]{:S(2)}) collective-permute-start(bf16[2,256,256]{1,2,0:T(8,128)(2,1)} %get-tuple-element.19), channel_id=1, source_target_pairs={{0,16},{1,17},{2,18},{3,19},{4,20},{5,21},{6,22},{7,23},{8,24},{9,... | collective-permute-start | bytes 786440 | tf_op jit(solution)/shard_map/ppermute | solution.py:23
  148.7 13.3 %copy-start.19 = (f32[128]{0:T(128)S(1)}, f32[128]{0:T(128)}, u32[]{:S(2)}) copy-start(f32[128]{0:T(128)} %copy-done.18) | copy-start | bytes 1540
  158.4 14.6 %collective-permute-start.5 = (bf16[9,2,256,256]{2,3,1,0:T(8,128)(2,1)}, bf16[9,2,256,256]{2,3,1,0:T(8,128)(2,1)}, u32[]{:S(2)}, u32[]{:S(2)}) collective-permute-start(bf16[9,2,256,256]{2,3,1,0:T(8,128)(2,1)} %bitcast_dynamic-update-slice_fusion), channel_id=1, source_target_pairs={{0,1},{1,0},{2,3},{3,2},{4,5},{5,4},{6,7},{7,6},{8,9},{9,8},{10,11... | collective-permute-start | bytes 7077896 | tf_op jit(solution)/shard_map/ppermute | solution.py:17
  185.3 41.2 %copy-start.7 = (bf16[256,320]{0,1:T(8,128)(2,1)S(1)}, bf16[256,320]{0,1:T(8,128)(2,1)}, u32[]{:S(2)}) copy-start(bf16[256,320]{0,1:T(8,128)(2,1)} %param.12) | copy-start | bytes 491524
  186.4 40.2 %all-to-all-start.1 = ((bf16[8,256,256]{2,1,0:T(8,128)(2,1)}), bf16[8,256,256]{2,1,0:T(8,128)(2,1)S(1)}, u32[]{:S(2)}, u32[]{:S(2)}) async-start(bf16[8,256,256]{2,1,0:T(8,128)(2,1)} %broadcast_in_dim.45), calls=%async_computation.1 | async-start | bytes 2097152 | tf_op jit(solution)/shard_map/all_to_all | solution.py:35
  229.0 9.9 %all-to-all-start.3 = ((f32[8,4,256]{2,1,0:T(4,128)}), f32[8,4,256]{2,1,0:T(4,128)S(1)}, u32[]{:S(2)}, u32[]{:S(2)}) async-start(f32[8,4,256]{2,1,0:T(4,128)} %broadcast_in_dim.46), calls=%async_computation.3 | async-start | bytes 65536 | tf_op jit(solution)/shard_map/all_to_all | solution.py:35
  240.3 20.2 %all-to-all-start.4 = ((bf16[8,256,320]{1,2,0:T(8,128)(2,1)}), bf16[8,256,320]{1,2,0:T(8,128)(2,1)S(1)}, u32[]{:S(2)}, u32[]{:S(2)}) async-start(bf16[8,256,320]{1,2,0:T(8,128)(2,1)} %broadcast_in_dim.47), calls=%async_computation.4 | async-start | bytes 2621440 | tf_op jit(solution)/shard_map/all_to_all | solution.py:35
  244.7 20.5 %copy-start.10 = (bf16[2,128,256]{2,1,0:T(8,128)(2,1)}, bf16[2,128,256]{2,1,0:T(8,128)(2,1)S(1)}, u32[]{:S(2)}) copy-start(bf16[2,128,256]{2,1,0:T(8,128)(2,1)S(1)} %scatter_fusion) | copy-start | bytes 393220
  (17 other events, 79.6 us)
Sparse Core Ops, SparseCore 0:
  19.7 131.3 all-gather.1

commit v2 on v1

--- a/solution.py
+++ b/solution.py
@@ -121,10 +121,13 @@
     page_cache = jnp.zeros_like(page_rows).at[page_slots].set(page_rows)
     key_block = jnp.stack([keys_full, values_full])
     half_span = span_blocks // 2
-    series = key_block[None]
-    while series.shape[0] < half_span:
-        received = shifted(series, "seq", 2 * series.shape[0])
-        series = jnp.concatenate([series, received], axis=0)
+    near_blocks = half_span // 2
+    near = [key_block]
+    for step in range(1, near_blocks):
+        near.append(shifted(key_block, "seq", 2 * step))
+    series = jnp.stack(near)
+    received = shifted(series, "seq", 2 * near_blocks)
+    series = jnp.concatenate([series, received], axis=0)
     series = jnp.concatenate([series, shifted(key_block, "seq", 2 * half_span)[None]], axis=0)
     partner = swapped(series, "seq", 0)
     parity = lax.axis_index("seq") % 2

time: 274 us -> 236 us (0.86)
  the two profiles are of different devices: /device:TPU:48 before, /device:TPU:168 now
where the time goes in v2:
time: 236 us; the launch traced here: 235 us
  waiting for transfers between devices  113 us (48%)
  starting transfers between devices  49.4 us (21%)
  local copies, waits for them, and re-layouts  31.8 us (13%)
  matrix products  15.1 us (6%)
  between operations  14.6 us (6%)
  other arithmetic  11 us (5%)
    ppermute x5, waiting for transfers between devices, shifted(): return lax.ppermute(block, axis, route)  56.2 us
    all_to_all x4, waiting for transfers between devices, group_parts(): return lax.all_to_all(spread, GROUP, 0, 0, tiled=True)  52.3 us
    ppermute x5, starting transfers between devices, shifted(): return lax.ppermute(block, axis, route)  23.4 us
    all_to_all x4, starting transfers between devices, group_parts(): return lax.all_to_all(spread, GROUP, 0, 0, tiled=True)  17 us
    unnamed x64, local copies, waits for them, and re-layouts  10.2 us
    slice x3, local copies, waits for them, and re-layouts, part_scores(): keys = stack[:, 0].reshape(-1, head_width)  7.66 us
    dot_general x2, matrix products, part_scores(): lax.dot_general(queries, keys, (((1,), (1,)), ((), ())), preferred_elemen...  5.97 us
    broadcast_in_dim x4, local copies, waits for them, and re-layouts, group_parts(): spread = jnp.broadcast_to(value[None], (group_count(),) + value.shape)  4.96 us
  transfers between devices with their start and end apart: 13, of which 8 were waited for; matrix products, arithmetic and copies ran while one was open for 20% of the time, Pallas kernels for 0%

profile of v2, /device:TPU:168, one launch (start us, length us, event | category | flops | bytes accessed | tf_op | source)
XLA Modules:
  0.0 234.7 jit_solution(15928747990226889062)
XLA Ops:
  9.4 6.2 %all-to-all-start = ((bf16[8,256,320]{1,2,0:T(8,128)(2,1)}), bf16[8,256,320]{1,2,0:T(8,128)(2,1)S(1)}, u32[]{:S(2)}, u32[]{:S(2)}) async-start(bf16[8,256,320]{1,2,0:T(8,128)(2,1)} %broadcast_in_dim.36), calls=%async_computation | async-start | bytes 2621440 | tf_op jit(solution)/shard_map/all_to_all | solution.py:35
  17.1 16.2 %all-to-all-done = bf16[8,256,320]{1,2,0:T(8,128)(2,1)S(1)} async-done(((bf16[8,256,320]{1,2,0:T(8,128)(2,1)}), bf16[8,256,320]{1,2,0:T(8,128)(2,1)S(1)}, u32[]{:S(2)}, u32[]{:S(2)}) %all-to-all-start) | async-done | bytes 1310752 | tf_op jit(solution)/shard_map/all_to_all | solution.py:35
  35.8 2.8 %collective-permute-start = (bf16[256,256]{0,1:T(8,128)(2,1)S(1)}, bf16[256,256]{0,1:T(8,128)(2,1)S(1)}, u32[]{:S(2)}, u32[]{:S(2)}) collective-permute-start(bf16[256,256]{0,1:T(8,128)(2,1)S(1)} %convolution_convert_fusion), channel_id=1, source_target_pairs={{0,64},{64,0},{128,192},{192,128},{1,65},{65,1},{129,193},{193,129... | collective-permute-start | bytes 393224 | tf_op jit(solution)/shard_map/ppermute | solution.py:17
  38.6 4.2 %collective-permute-done = bf16[256,256]{0,1:T(8,128)(2,1)S(1)} collective-permute-done((bf16[256,256]{0,1:T(8,128)(2,1)S(1)}, bf16[256,256]{0,1:T(8,128)(2,1)S(1)}, u32[]{:S(2)}, u32[]{:S(2)}) %collective-permute-start) | collective-permute-done | bytes 131104 | tf_op jit(solution)/shard_map/ppermute | solution.py:17
  46.9 6.4 %collective-permute-start.1 = (bf16[2,256,256]{1,2,0:T(8,128)(2,1)}, bf16[2,256,256]{1,2,0:T(8,128)(2,1)S(1)}, u32[]{:S(2)}, u32[]{:S(2)}) collective-permute-start(bf16[2,256,256]{1,2,0:T(8,128)(2,1)} %get-tuple-element.20), channel_id=1, source_target_pairs={{0,2},{1,3},{2,4},{3,5},{4,6},{5,7},{6,8},{7,9},{8,10},{9,11},{10,... | collective-permute-start | bytes 786440 | tf_op jit(solution)/shard_map/ppermute | solution.py:23
  53.3 8.0 %collective-permute-start.2 = (bf16[2,256,256]{1,2,0:T(8,128)(2,1)}, bf16[2,256,256]{1,2,0:T(8,128)(2,1)}, u32[]{:S(2)}, u32[]{:S(2)}) collective-permute-start(bf16[2,256,256]{1,2,0:T(8,128)(2,1)} %get-tuple-element.20), channel_id=1, source_target_pairs={{0,4},{1,5},{2,6},{3,7},{4,8},{5,9},{6,10},{7,11},{8,12},{9,13},{1... | collective-permute-start | bytes 786440 | tf_op jit(solution)/shard_map/ppermute | solution.py:23
  62.8 4.3 %all-to-all-start.2 = ((bf16[256,8,320]{0,2,1:T(8,128)(2,1)}), bf16[256,8,320]{0,2,1:T(8,128)(2,1)}, u32[]{:S(2)}, u32[]{:S(2)}) async-start(bf16[256,8,320]{0,2,1:T(8,128)(2,1)} %bitcast.17), calls=%async_computation.2 | async-start | bytes 2621440 | tf_op jit(solution)/shard_map/all_to_all | solution.py:95
  67.7 18.2 %collective-permute-done.2 = bf16[2,256,256]{1,2,0:T(8,128)(2,1)} collective-permute-done((bf16[2,256,256]{1,2,0:T(8,128)(2,1)}, bf16[2,256,256]{1,2,0:T(8,128)(2,1)}, u32[]{:S(2)}, u32[]{:S(2)}) %collective-permute-start.2) | collective-permute-done | bytes 262176 | tf_op jit(solution)/shard_map/ppermute | solution.py:23
  87.9 2.5 %collective-permute-start.4 = (bf16[4,2,256,256]{2,3,1,0:T(8,128)(2,1)}, bf16[4,2,256,256]{2,3,1,0:T(8,128)(2,1)}, u32[]{:S(2)}, u32[]{:S(2)}) collective-permute-start(bf16[4,2,256,256]{2,3,1,0:T(8,128)(2,1)} %pad_maximum_fusion), channel_id=1, source_target_pairs={{0,8},{1,9},{2,10},{3,11},{4,12},{5,13},{6,14},{7,15},{8,16},{9,17... | collective-permute-start | bytes 3145736 | tf_op jit(solution)/shard_map/ppermute | solution.py:23
  90.5 4.6 %collective-permute-start.5 = (bf16[2,256,256]{1,2,0:T(8,128)(2,1)}, bf16[2,256,256]{1,2,0:T(8,128)(2,1)S(1)}, u32[]{:S(2)}, u32[]{:S(2)}) collective-permute-start(bf16[2,256,256]{1,2,0:T(8,128)(2,1)} %get-tuple-element.20), channel_id=1, source_target_pairs={{0,16},{1,17},{2,18},{3,19},{4,20},{5,21},{6,22},{7,23},{8,24},{9,... | collective-permute-start | bytes 786440 | tf_op jit(solution)/shard_map/ppermute | solution.py:23
  99.8 29.7 %collective-permute-done.4 = bf16[4,2,256,256]{2,3,1,0:T(8,128)(2,1)} collective-permute-done((bf16[4,2,256,256]{2,3,1,0:T(8,128)(2,1)}, bf16[4,2,256,256]{2,3,1,0:T(8,128)(2,1)}, u32[]{:S(2)}, u32[]{:S(2)}) %collective-permute-start.4) | collective-permute-done | bytes 1048608 | tf_op jit(solution)/shard_map/ppermute | solution.py:23
  131.9 8.4 %collective-permute-done.5 = bf16[2,256,256]{1,2,0:T(8,128)(2,1)S(1)} collective-permute-done((bf16[2,256,256]{1,2,0:T(8,128)(2,1)}, bf16[2,256,256]{1,2,0:T(8,128)(2,1)S(1)}, u32[]{:S(2)}, u32[]{:S(2)}) %collective-permute-start.5) | collective-permute-done | bytes 262176 | tf_op jit(solution)/shard_map/ppermute | solution.py:23
  145.1 2.8 %fusion.57 = (bf16[9,1,256,256]{2,3,1,0:T(8,128)(2,1)}, bf16[9,1,256,256]{2,3,1,0:T(8,128)(2,1)S(1)}) fusion(bf16[9,2,256,256]{2,3,1,0:T(8,128)(2,1)} %bitcast_dynamic-update-slice_fusion), kind=kLoop, calls=%fused_computation.112 | loop fusion | bytes 4718592 | tf_op jit(solution)/shard_map/slice | solution.py:146
  147.9 2.4 %copy.30 = bf16[9,1,256,256]{3,2,0,1:T(8,128)(2,1)} copy(bf16[9,1,256,256]{2,3,1,0:T(8,128)(2,1)} %get-tuple-element.15) | data formatting | bytes 2359296 | tf_op jit(solution)/shard_map/slice | solution.py:146
  151.9 3.6 %fusion.61 = (f32[256]{0:T(256)S(1)}, f32[256,2304]{1,0:T(8,128)}) fusion(bf16[2304,256]{1,0:T(8,128)(2,1)} %bitcast.73, bf16[256,128]{0,1:T(8,128)(2,1)S(1)} %get-tuple-element.18, bf16[256,128]{0,1:T(8,128)(2,1)S(1)} %get-tuple-element.17, s32[256]{0:T(256)S(1)} %copy-done.25, s32[2304]{0:T(1024)S(1)} %add.186, s32[256]{0:T(256)S(1)} %copy-done.17, ...), kind=kOutput, calls=%fused_computation.116 | convolution fusion | flops 305790720 | bytes 3691520 | tf_op jit(solution)/shard_map/dot_general | solution.py:147
  155.5 2.8 %fusion.56 = (bf16[9,1,256,256]{2,3,1,0:T(8,128)(2,1)S(1)}, bf16[9,1,256,256]{2,3,1,0:T(8,128)(2,1)}) fusion(bf16[9,2,256,256]{2,3,1,0:T(8,128)(2,1)} %collective-permute-done.6), kind=kLoop, calls=%fused_computation.111 | loop fusion | bytes 4718592 | tf_op jit(solution)/shard_map/slice | solution.py:165
  158.3 2.4 %copy.31 = bf16[9,1,256,256]{3,2,0,1:T(8,128)(2,1)} copy(bf16[9,1,256,256]{2,3,1,0:T(8,128)(2,1)} %get-tuple-element.14) | data formatting | bytes 2359296 | tf_op jit(solution)/shard_map/slice | solution.py:146
  168.9 3.6 %all-to-all-start.1 = ((bf16[8,256,256]{2,1,0:T(8,128)(2,1)}), bf16[8,256,256]{2,1,0:T(8,128)(2,1)S(1)}, u32[]{:S(2)}, u32[]{:S(2)}) async-start(bf16[8,256,256]{2,1,0:T(8,128)(2,1)} %broadcast_in_dim.42), calls=%async_computation.1 | async-start | bytes 2097152 | tf_op jit(solution)/shard_map/all_to_all | solution.py:35
  173.2 14.9 %all-to-all-done.1 = bf16[8,256,256]{2,1,0:T(8,128)(2,1)S(1)} async-done(((bf16[8,256,256]{2,1,0:T(8,128)(2,1)}), bf16[8,256,256]{2,1,0:T(8,128)(2,1)S(1)}, u32[]{:S(2)}, u32[]{:S(2)}) %all-to-all-start.1) | async-done | bytes 1048608 | tf_op jit(solution)/shard_map/all_to_all | solution.py:35
  190.6 3.6 %all-to-all-start.3 = ((f32[8,4,256]{2,1,0:T(4,128)}), f32[8,4,256]{2,1,0:T(4,128)S(1)}, u32[]{:S(2)}, u32[]{:S(2)}) async-start(f32[8,4,256]{2,1,0:T(4,128)} %broadcast_in_dim.43), calls=%async_computation.3 | async-start | bytes 65536 | tf_op jit(solution)/shard_map/all_to_all | solution.py:35
  195.0 5.5 %all-to-all-done.3 = f32[8,4,256]{2,1,0:T(4,128)S(1)} async-done(((f32[8,4,256]{2,1,0:T(4,128)}), f32[8,4,256]{2,1,0:T(4,128)S(1)}, u32[]{:S(2)}, u32[]{:S(2)}) %all-to-all-start.3) | async-done | bytes 32800 | tf_op jit(solution)/shard_map/all_to_all | solution.py:35
  201.9 3.6 %all-to-all-start.4 = ((bf16[8,256,320]{1,2,0:T(8,128)(2,1)}), bf16[8,256,320]{1,2,0:T(8,128)(2,1)S(1)}, u32[]{:S(2)}, u32[]{:S(2)}) async-start(bf16[8,256,320]{1,2,0:T(8,128)(2,1)} %broadcast_in_dim.44), calls=%async_computation.4 | async-start | bytes 2621440 | tf_op jit(solution)/shard_map/all_to_all | solution.py:35
  206.3 15.8 %all-to-all-done.4 = bf16[8,256,320]{1,2,0:T(8,128)(2,1)S(1)} async-done(((bf16[8,256,320]{1,2,0:T(8,128)(2,1)}), bf16[8,256,320]{1,2,0:T(8,128)(2,1)S(1)}, u32[]{:S(2)}, u32[]{:S(2)}) %all-to-all-start.4) | async-done | bytes 1310752 | tf_op jit(solution)/shard_map/all_to_all | solution.py:35
  222.1 4.8 %fusion.63 = f32[256,1280]{1,0:T(8,128)S(1)} fusion(bf16[256,2560]{0,1:T(8,128)(2,1)S(1)} %bitcast.69, bf16[2560,1280]{1,0:T(8,128)(2,1)} %all-gather.2.cloned.1.call-done), kind=kOutput, calls=%fused_computation.118 | convolution fusion | flops 1677721600 | bytes 9175040 | tf_op jit(solution)/shard_map/dot_general | solution.py:199
  (134 shorter events, 43.0 us)
Async XLA Ops:
  7.2 136.5 %copy-start = (bf16[2560,256]{1,0:T(8,128)(2,1)S(1)}, bf16[2560,256]{1,0:T(8,128)(2,1)}, u32[]{:S(2)}) copy-start(bf16[2560,256]{1,0:T(8,128)(2,1)} %param.13) | copy-start | bytes 3932164
  9.4 24.2 %copy-start.15 = (f32[2560]{0:T(1024)S(1)}, f32[2560]{0:T(1024)}, u32[]{:S(2)}) copy-start(f32[2560]{0:T(1024)} %param.17) | copy-start | bytes 30724
  9.4 23.8 %all-to-all-start = ((bf16[8,256,320]{1,2,0:T(8,128)(2,1)}), bf16[8,256,320]{1,2,0:T(8,128)(2,1)S(1)}, u32[]{:S(2)}, u32[]{:S(2)}) async-start(bf16[8,256,320]{1,2,0:T(8,128)(2,1)} %broadcast_in_dim.36), calls=%async_computation | async-start | bytes 2621440 | tf_op jit(solution)/shard_map/all_to_all | solution.py:35
  15.6 206.5 %all-gather.2.cloned.1.call-start = ((), (), s32[]{:S(2)}) async-start(), calls=%async_computation.5 | async-start | bytes 6656000 | tf_op jit(solution)/shard_map/all_gather | solution.py:196
  16.5 17.1 %copy-start.24 = (s32[256]{0:T(256)}, s32[256]{0:T(256)S(1)}, u32[]{:S(2)}) copy-start(s32[256]{0:T(256)S(1)} %iota_add_fusion.2) | copy-start | bytes 3076
  16.6 16.6 %copy-start.16 = (s32[256]{0:T(256)}, s32[256]{0:T(256)S(1)}, u32[]{:S(2)}) copy-start(s32[256]{0:T(256)S(1)} %convert_reduce_fusion.2) | copy-start | bytes 3076
  35.1 26.2 %copy-start.2 = (bf16[256,2560]{1,0:T(8,128)(2,1)S(1)}, bf16[256,2560]{1,0:T(8,128)(2,1)}, u32[]{:S(2)}) copy-start(bf16[256,2560]{1,0:T(8,128)(2,1)} %param.15) | copy-start | bytes 3932164
  35.8 7.0 %collective-permute-start = (bf16[256,256]{0,1:T(8,128)(2,1)S(1)}, bf16[256,256]{0,1:T(8,128)(2,1)S(1)}, u32[]{:S(2)}, u32[]{:S(2)}) collective-permute-start(bf16[256,256]{0,1:T(8,128)(2,1)S(1)} %convolution_convert_fusion), channel_id=1, source_target_pairs={{0,64},{64,0},{128,192},{192,128},{1,65},{65,1},{129,193},{193,129... | collective-permute-start | bytes 393224 | tf_op jit(solution)/shard_map/ppermute | solution.py:17
  45.0 22.7 %collective-permute-start.3 = (bf16[2,256,256]{1,2,0:T(8,128)(2,1)}, bf16[2,256,256]{1,2,0:T(8,128)(2,1)S(1)}, u32[]{:S(2)}, u32[]{:S(2)}) collective-permute-start(bf16[2,256,256]{1,2,0:T(8,128)(2,1)} %get-tuple-element.20), channel_id=1, source_target_pairs={{0,6},{1,7},{2,8},{3,9},{4,10},{5,11},{6,12},{7,13},{8,14},{9,15},... | collective-permute-start | bytes 786440 | tf_op jit(solution)/shard_map/ppermute | solution.py:23
  46.9 20.7 %collective-permute-start.1 = (bf16[2,256,256]{1,2,0:T(8,128)(2,1)}, bf16[2,256,256]{1,2,0:T(8,128)(2,1)S(1)}, u32[]{:S(2)}, u32[]{:S(2)}) collective-permute-start(bf16[2,256,256]{1,2,0:T(8,128)(2,1)} %get-tuple-element.20), channel_id=1, source_target_pairs={{0,2},{1,3},{2,4},{3,5},{4,6},{5,7},{6,8},{7,9},{8,10},{9,11},{10,... | collective-permute-start | bytes 786440 | tf_op jit(solution)/shard_map/ppermute | solution.py:23
  53.3 32.5 %collective-permute-start.2 = (bf16[2,256,256]{1,2,0:T(8,128)(2,1)}, bf16[2,256,256]{1,2,0:T(8,128)(2,1)}, u32[]{:S(2)}, u32[]{:S(2)}) collective-permute-start(bf16[2,256,256]{1,2,0:T(8,128)(2,1)} %get-tuple-element.20), channel_id=1, source_target_pairs={{0,4},{1,5},{2,6},{3,7},{4,8},{5,9},{6,10},{7,11},{8,12},{9,13},{1... | collective-permute-start | bytes 786440 | tf_op jit(solution)/shard_map/ppermute | solution.py:23
  62.8 105.1 %all-to-all-start.2 = ((bf16[256,8,320]{0,2,1:T(8,128)(2,1)}), bf16[256,8,320]{0,2,1:T(8,128)(2,1)}, u32[]{:S(2)}, u32[]{:S(2)}) async-start(bf16[256,8,320]{0,2,1:T(8,128)(2,1)} %bitcast.17), calls=%async_computation.2 | async-start | bytes 2621440 | tf_op jit(solution)/shard_map/all_to_all | solution.py:95
  87.9 41.6 %collective-permute-start.4 = (bf16[4,2,256,256]{2,3,1,0:T(8,128)(2,1)}, bf16[4,2,256,256]{2,3,1,0:T(8,128)(2,1)}, u32[]{:S(2)}, u32[]{:S(2)}) collective-permute-start(bf16[4,2,256,256]{2,3,1,0:T(8,128)(2,1)} %pad_maximum_fusion), channel_id=1, source_target_pairs={{0,8},{1,9},{2,10},{3,11},{4,12},{5,13},{6,14},{7,15},{8,16},{9,17... | collective-permute-start | bytes 3145736 | tf_op jit(solution)/shard_map/ppermute | solution.py:23
  90.5 52.3 %copy-start.21 = (s32[9]{0:T(128)S(1)}, s32[9]{0:T(128)}, u32[]{:S(2)}) copy-start(s32[9]{0:T(128)} %get-tuple-element.40) | copy-start | bytes 112
  90.5 53.2 %copy-start.4 = (bf16[256,2560]{0,1:T(8,128)(2,1)S(1)}, bf16[256,2560]{0,1:T(8,128)(2,1)}, u32[]{:S(2)}) copy-start(bf16[256,2560]{0,1:T(8,128)(2,1)} %copy-done.3) | copy-start | bytes 3932164
  90.5 49.7 %collective-permute-start.5 = (bf16[2,256,256]{1,2,0:T(8,128)(2,1)}, bf16[2,256,256]{1,2,0:T(8,128)(2,1)S(1)}, u32[]{:S(2)}, u32[]{:S(2)}) collective-permute-start(bf16[2,256,256]{1,2,0:T(8,128)(2,1)} %get-tuple-element.20), channel_id=1, source_target_pairs={{0,16},{1,17},{2,18},{3,19},{4,20},{5,21},{6,22},{7,23},{8,24},{9,... | collective-permute-start | bytes 786440 | tf_op jit(solution)/shard_map/ppermute | solution.py:23
  131.9 12.5 %copy-start.23 = (f32[256]{0:T(256)S(1)}, f32[256]{0:T(256)}, u32[]{:S(2)}) copy-start(f32[256]{0:T(256)} %param.20) | copy-start | bytes 3076
  131.9 12.6 %copy-start.19 = (f32[128]{0:T(128)S(1)}, f32[128]{0:T(128)}, u32[]{:S(2)}) copy-start(f32[128]{0:T(128)} %copy-done.18) | copy-start | bytes 1540
  140.9 14.5 %collective-permute-start.6 = (bf16[9,2,256,256]{2,3,1,0:T(8,128)(2,1)}, bf16[9,2,256,256]{2,3,1,0:T(8,128)(2,1)}, u32[]{:S(2)}, u32[]{:S(2)}) collective-permute-start(bf16[9,2,256,256]{2,3,1,0:T(8,128)(2,1)} %bitcast_dynamic-update-slice_fusion), channel_id=1, source_target_pairs={{0,1},{1,0},{2,3},{3,2},{4,5},{5,4},{6,7},{7,6},{8,9},{9,8},{10,11... | collective-permute-start | bytes 7077896 | tf_op jit(solution)/shard_map/ppermute | solution.py:17
  167.8 20.3 %copy-start.7 = (bf16[256,320]{0,1:T(8,128)(2,1)S(1)}, bf16[256,320]{0,1:T(8,128)(2,1)}, u32[]{:S(2)}) copy-start(bf16[256,320]{0,1:T(8,128)(2,1)} %param.12) | copy-start | bytes 491524
  168.9 19.2 %all-to-all-start.1 = ((bf16[8,256,256]{2,1,0:T(8,128)(2,1)}), bf16[8,256,256]{2,1,0:T(8,128)(2,1)S(1)}, u32[]{:S(2)}, u32[]{:S(2)}) async-start(bf16[8,256,256]{2,1,0:T(8,128)(2,1)} %broadcast_in_dim.42), calls=%async_computation.1 | async-start | bytes 2097152 | tf_op jit(solution)/shard_map/all_to_all | solution.py:35
  190.6 9.9 %all-to-all-start.3 = ((f32[8,4,256]{2,1,0:T(4,128)}), f32[8,4,256]{2,1,0:T(4,128)S(1)}, u32[]{:S(2)}, u32[]{:S(2)}) async-start(f32[8,4,256]{2,1,0:T(4,128)} %broadcast_in_dim.43), calls=%async_computation.3 | async-start | bytes 65536 | tf_op jit(solution)/shard_map/all_to_all | solution.py:35
  201.9 20.2 %all-to-all-start.4 = ((bf16[8,256,320]{1,2,0:T(8,128)(2,1)}), bf16[8,256,320]{1,2,0:T(8,128)(2,1)S(1)}, u32[]{:S(2)}, u32[]{:S(2)}) async-start(bf16[8,256,320]{1,2,0:T(8,128)(2,1)} %broadcast_in_dim.44), calls=%async_computation.4 | async-start | bytes 2621440 | tf_op jit(solution)/shard_map/all_to_all | solution.py:35
  206.3 20.6 %copy-start.10 = (bf16[2,128,256]{2,1,0:T(8,128)(2,1)}, bf16[2,128,256]{2,1,0:T(8,128)(2,1)S(1)}, u32[]{:S(2)}) copy-start(bf16[2,128,256]{2,1,0:T(8,128)(2,1)S(1)} %scatter_fusion) | copy-start | bytes 393220
  (18 other events, 72.8 us)
Sparse Core Ops, SparseCore 0:
  19.7 120.5 all-gather.1

commit v3 on v2

--- a/solution.py
+++ b/solution.py
@@ -39,10 +39,6 @@
     rows, width = block.shape
     parts = group_parts(block)
     return parts.transpose(1, 0, 2).reshape(rows, parts.shape[0] * width)
-
-
-def group_sum(vector):
-    return jnp.sum(group_parts(vector), axis=0)
 
 
 def rms_norm(values, weights):
@@ -166,33 +162,10 @@
         )
     ).astype(jnp.bfloat16)
     all_heads = group_gather(attention_out)
-    attended = jnp.dot(all_heads, out_columns, preferred_element_type=jnp.float32)
-    width = attended.shape[1]
-    first_column = lax.axis_index(GROUP) * width
-    post_local = lax.dynamic_slice_in_dim(post_gain, first_column, width)
-    mlp_local = lax.dynamic_slice_in_dim(mlp_gain, first_column, width)
-    model_width = features.shape[1]
-    token_rows = tokens.astype(jnp.float32)
-    scaled = attended * post_local
-    sums = group_sum(
-        jnp.stack(
-            [
-                jnp.sum(attended * attended, axis=1),
-                jnp.sum(token_rows * token_rows, axis=1),
-                jnp.sum(token_rows * scaled, axis=1),
-                jnp.sum(scaled * scaled, axis=1),
-            ]
-        )
-    )
-    attended_inverse = lax.rsqrt(sums[0] / model_width + NORM_EPS)
-    residual = token_rows + attended * attended_inverse[:, None] * post_local
-    residual_square = jnp.maximum(
-        sums[1] + 2.0 * attended_inverse * sums[2] + attended_inverse * attended_inverse * sums[3],
-        0.0,
-    )
-    residual_inverse = lax.rsqrt(residual_square / model_width + NORM_EPS)
-    ffn_local = (residual * residual_inverse[:, None] * mlp_local).astype(jnp.bfloat16)
-    ffn_input = group_gather(ffn_local)
+    attended_local = jnp.dot(all_heads, out_columns, preferred_element_type=jnp.float32)
+    attended = group_gather(attended_local.astype(jnp.bfloat16))
+    residual = features.astype(jnp.float32) + rms_norm(attended, post_gain)
+    ffn_input = rms_norm(residual, mlp_gain).astype(jnp.bfloat16)
     row_piece = lax.all_gather(
         w_gateup.reshape(w_gateup.shape[0], 2 * unit_count), "seq", axis=0, tiled=True
     )

time: 236 us -> 241 us (1.021)
  the two profiles are of different devices: /device:TPU:168 before, /device:TPU:40 now
where the time goes in v3:
time: 241 us; the launch traced here: 240 us
  waiting for transfers between devices  92 us (38%)
  starting transfers between devices  41.1 us (17%)
  local copies, waits for them, and re-layouts  32.7 us (14%)
  blocking collectives  25.2 us (10%)
  other arithmetic  17.9 us (7%)
  matrix products  16.7 us (7%)
  between operations  14.6 us (6%)
    ppermute x5, waiting for transfers between devices, shifted(): return lax.ppermute(block, axis, route)  56.3 us
    all_to_all x2, waiting for transfers between devices, group_parts(): return lax.all_to_all(spread, GROUP, 0, 0, tiled=True)  31.4 us
    all_to_all x1, blocking collectives, group_parts(): return lax.all_to_all(spread, GROUP, 0, 0, tiled=True)  25.2 us
    ppermute x5, starting transfers between devices, shifted(): return lax.ppermute(block, axis, route)  21.5 us
    unnamed x62, local copies, waits for them, and re-layouts  11.5 us
    all_to_all x2, starting transfers between devices, group_parts(): return lax.all_to_all(spread, GROUP, 0, 0, tiled=True)  10.7 us
    slice x3, local copies, waits for them, and re-layouts, part_scores(): keys = stack[:, 0].reshape(-1, head_width)  8.04 us
    dot_general x2, matrix products, part_scores(): lax.dot_general(queries, keys, (((1,), (1,)), ((), ())), preferred_elemen...  5.94 us
  transfers between devices with their start and end apart: 11, of which 7 were waited for; matrix products, arithmetic and copies ran while one was open for 23% of the time, Pallas kernels for 0%

profile of v3, /device:TPU:40, one launch (start us, length us, event | category | flops | bytes accessed | tf_op | source)
XLA Modules:
  0.0 240.2 jit_solution(10310914572774340056)
XLA Ops:
  9.4 6.2 %all-to-all-start = ((bf16[8,256,320]{1,2,0:T(8,128)(2,1)}), bf16[8,256,320]{1,2,0:T(8,128)(2,1)S(1)}, u32[]{:S(2)}, u32[]{:S(2)}) async-start(bf16[8,256,320]{1,2,0:T(8,128)(2,1)} %broadcast_in_dim.33), calls=%async_computation | async-start | bytes 2621440 | tf_op jit(solution)/shard_map/all_to_all | solution.py:35
  17.3 15.9 %all-to-all-done = bf16[8,256,320]{1,2,0:T(8,128)(2,1)S(1)} async-done(((bf16[8,256,320]{1,2,0:T(8,128)(2,1)}), bf16[8,256,320]{1,2,0:T(8,128)(2,1)S(1)}, u32[]{:S(2)}, u32[]{:S(2)}) %all-to-all-start) | async-done | bytes 1310752 | tf_op jit(solution)/shard_map/all_to_all | solution.py:35
  35.8 2.8 %collective-permute-start = (bf16[256,256]{0,1:T(8,128)(2,1)S(1)}, bf16[256,256]{0,1:T(8,128)(2,1)S(1)}, u32[]{:S(2)}, u32[]{:S(2)}) collective-permute-start(bf16[256,256]{0,1:T(8,128)(2,1)S(1)} %convolution_convert_fusion), channel_id=1, source_target_pairs={{0,64},{64,0},{128,192},{192,128},{1,65},{65,1},{129,193},{193,129... | collective-permute-start | bytes 393224 | tf_op jit(solution)/shard_map/ppermute | solution.py:17
  38.6 4.2 %collective-permute-done = bf16[256,256]{0,1:T(8,128)(2,1)S(1)} collective-permute-done((bf16[256,256]{0,1:T(8,128)(2,1)S(1)}, bf16[256,256]{0,1:T(8,128)(2,1)S(1)}, u32[]{:S(2)}, u32[]{:S(2)}) %collective-permute-start) | collective-permute-done | bytes 131104 | tf_op jit(solution)/shard_map/ppermute | solution.py:17
  45.0 10.0 %collective-permute-start.2 = (bf16[2,256,256]{1,2,0:T(8,128)(2,1)}, bf16[2,256,256]{1,2,0:T(8,128)(2,1)S(1)}, u32[]{:S(2)}, u32[]{:S(2)}) collective-permute-start(bf16[2,256,256]{1,2,0:T(8,128)(2,1)} %get-tuple-element.16), channel_id=1, source_target_pairs={{0,4},{1,5},{2,6},{3,7},{4,8},{5,9},{6,10},{7,11},{8,12},{9,13},{1... | collective-permute-start | bytes 786440 | tf_op jit(solution)/shard_map/ppermute | solution.py:23
  57.0 4.9 %collective-permute-start.1 = (bf16[2,256,256]{1,2,0:T(8,128)(2,1)}, bf16[2,256,256]{1,2,0:T(8,128)(2,1)}, u32[]{:S(2)}, u32[]{:S(2)}) collective-permute-start(bf16[2,256,256]{1,2,0:T(8,128)(2,1)} %get-tuple-element.16), channel_id=1, source_target_pairs={{0,2},{1,3},{2,4},{3,5},{4,6},{5,7},{6,8},{7,9},{8,10},{9,11},{10,... | collective-permute-start | bytes 786440 | tf_op jit(solution)/shard_map/ppermute | solution.py:23
  61.9 2.5 %copy.28 = bf16[256,2560]{0,1:T(8,128)(2,1)} copy(bf16[256,2560]{1,0:T(8,128)(2,1)} %param.15) | data formatting | bytes 2621440 | tf_op args[3]
  64.4 4.3 %all-to-all-start.2 = ((bf16[256,8,320]{0,2,1:T(8,128)(2,1)}), bf16[256,8,320]{0,2,1:T(8,128)(2,1)}, u32[]{:S(2)}, u32[]{:S(2)}) async-start(bf16[256,8,320]{0,2,1:T(8,128)(2,1)} %bitcast.73), calls=%async_computation.2 | async-start | bytes 2621440 | tf_op jit(solution)/shard_map/all_to_all | solution.py:91
  69.1 6.5 %collective-permute-done.3 = bf16[2,256,256]{1,2,0:T(8,128)(2,1)S(1)} collective-permute-done((bf16[2,256,256]{1,2,0:T(8,128)(2,1)}, bf16[2,256,256]{1,2,0:T(8,128)(2,1)S(1)}, u32[]{:S(2)}, u32[]{:S(2)}) %collective-permute-start.3) | collective-permute-done | bytes 262176 | tf_op jit(solution)/shard_map/ppermute | solution.py:23
  75.7 11.4 %collective-permute-done.1 = bf16[2,256,256]{1,2,0:T(8,128)(2,1)} collective-permute-done((bf16[2,256,256]{1,2,0:T(8,128)(2,1)}, bf16[2,256,256]{1,2,0:T(8,128)(2,1)}, u32[]{:S(2)}, u32[]{:S(2)}) %collective-permute-start.1) | collective-permute-done | bytes 262176 | tf_op jit(solution)/shard_map/ppermute | solution.py:23
  89.2 2.6 %collective-permute-start.4 = (bf16[4,2,256,256]{2,3,1,0:T(8,128)(2,1)}, bf16[4,2,256,256]{2,3,1,0:T(8,128)(2,1)}, u32[]{:S(2)}, u32[]{:S(2)}) collective-permute-start(bf16[4,2,256,256]{2,3,1,0:T(8,128)(2,1)} %pad_maximum_fusion), channel_id=1, source_target_pairs={{0,8},{1,9},{2,10},{3,11},{4,12},{5,13},{6,14},{7,15},{8,16},{9,17... | collective-permute-start | bytes 3145736 | tf_op jit(solution)/shard_map/ppermute | solution.py:23
  98.7 34.0 %collective-permute-done.4 = bf16[4,2,256,256]{2,3,1,0:T(8,128)(2,1)} collective-permute-done((bf16[4,2,256,256]{2,3,1,0:T(8,128)(2,1)}, bf16[4,2,256,256]{2,3,1,0:T(8,128)(2,1)}, u32[]{:S(2)}, u32[]{:S(2)}) %collective-permute-start.4) | collective-permute-done | bytes 1048608 | tf_op jit(solution)/shard_map/ppermute | solution.py:23
  135.0 4.4 %collective-permute-done.5 = bf16[2,256,256]{1,2,0:T(8,128)(2,1)S(1)} collective-permute-done((bf16[2,256,256]{1,2,0:T(8,128)(2,1)}, bf16[2,256,256]{1,2,0:T(8,128)(2,1)S(1)}, u32[]{:S(2)}, u32[]{:S(2)}) %collective-permute-start.5) | collective-permute-done | bytes 262176 | tf_op jit(solution)/shard_map/ppermute | solution.py:23
  145.6 3.3 %fusion.61 = (bf16[9,1,256,256]{2,3,1,0:T(8,128)(2,1)}, bf16[9,1,256,256]{2,3,1,0:T(8,128)(2,1)}) fusion(bf16[9,2,256,256]{2,3,1,0:T(8,128)(2,1)} %bitcast_dynamic-update-slice_fusion), kind=kLoop, calls=%fused_computation.111 | loop fusion | bytes 4718592 | tf_op jit(solution)/shard_map/slice | solution.py:142
  148.9 2.4 copy.24
  151.2 2.4 copy.26
  153.6 3.6 %fusion.64 = (f32[256]{0:T(256)S(1)}, f32[256,2304]{1,0:T(8,128)}) fusion(bf16[2304,256]{1,0:T(8,128)(2,1)} %bitcast.77, bf16[256,128]{0,1:T(8,128)(2,1)S(1)} %get-tuple-element.14, bf16[256,128]{0,1:T(8,128)(2,1)S(1)} %get-tuple-element.13, s32[256]{0:T(256)S(1)} %copy-done.24, s32[2304]{0:T(1024)S(1)} %add.166, s32[256]{0:T(256)S(1)} %copy-done.16, ...), kind=kOutput, calls=%fused_computation.114 | convolution fusion | flops 305790720 | bytes 3691520 | tf_op jit(solution)/shard_map/dot_general | solution.py:143
  157.2 3.4 %fusion.60 = (bf16[9,1,256,256]{2,3,1,0:T(8,128)(2,1)}, bf16[9,1,256,256]{2,3,1,0:T(8,128)(2,1)}) fusion(bf16[9,2,256,256]{2,3,1,0:T(8,128)(2,1)} %collective-permute-done.6), kind=kLoop, calls=%fused_computation.110 | loop fusion | bytes 4718592 | tf_op jit(solution)/shard_map/slice | solution.py:161
  162.9 2.4 copy.27
  171.0 25.2 %all_to_all.31 = bf16[8,256,256]{2,1,0:T(8,128)(2,1)S(1)} all-to-all(bf16[8,256,256]{2,1,0:T(8,128)(2,1)S(1)} %broadcast_in_dim.40), channel_id=1, replica_groups=mesh['section'=2,'tensor'=4,'seq'=64] {'section','tensor'}, dimensions={0} | all-to-all | bytes 2097152 | tf_op jit(solution)/shard_map/all_to_all | solution.py:35
  199.3 4.4 %all-to-all-start.3 = ((bf16[8,256,320]{1,2,0:T(8,128)(2,1)}), bf16[8,256,320]{1,2,0:T(8,128)(2,1)}, u32[]{:S(2)}, u32[]{:S(2)}) async-start(bf16[8,256,320]{1,2,0:T(8,128)(2,1)} %broadcast_in_dim.41), calls=%async_computation.3 | async-start | bytes 2621440 | tf_op jit(solution)/shard_map/all_to_all | solution.py:35
  204.6 15.5 %all-to-all-done.3 = bf16[8,256,320]{1,2,0:T(8,128)(2,1)} async-done(((bf16[8,256,320]{1,2,0:T(8,128)(2,1)}), bf16[8,256,320]{1,2,0:T(8,128)(2,1)}, u32[]{:S(2)}, u32[]{:S(2)}) %all-to-all-start.3) | async-done | bytes 1310752 | tf_op jit(solution)/shard_map/all_to_all | solution.py:35
  223.8 3.4 %fusion.6 = bf16[256,2560]{0,1:T(8,128)(2,1)} fusion(bf16[8,256,320]{1,2,0:T(8,128)(2,1)S(1)} %all-to-all-done, bf16[8,256,320]{1,2,0:T(8,128)(2,1)} %all-to-all-done.3, f32[2560]{0:T(1024)S(1)} %copy-done.14, f32[256]{0:T(256)S(1)} %add_rsqrt_fusion, f32[2560]{0:T(1024)S(1)} %copy-done.12, f32[256]{0:T(256)S(1)} %add_rsqrt_fusion.1), kind=kLoop, calls=%fused_computation.10 | loop fusion | flops 5242880 | bytes 3954688 | tf_op jit(solution)/shard_map/convert_element_type | solution.py:168
  227.3 5.2 %fusion.66 = f32[256,1280]{1,0:T(8,128)S(1)} fusion(bf16[256,2560]{0,1:T(8,128)(2,1)} %fusion.6, bf16[2560,1280]{1,0:T(8,128)(2,1)} %all-gather.2.cloned.1.call-done), kind=kOutput, calls=%fused_computation.116 | convolution fusion | flops 1677721600 | bytes 9175040 | tf_op jit(solution)/shard_map/dot_general | solution.py:172
  (127 shorter events, 44.9 us)
Async XLA Ops:
  7.2 135.7 %copy-start = (bf16[2560,256]{1,0:T(8,128)(2,1)S(1)}, bf16[2560,256]{1,0:T(8,128)(2,1)}, u32[]{:S(2)}) copy-start(bf16[2560,256]{1,0:T(8,128)(2,1)} %param.13) | copy-start | bytes 3932164
  7.2 8.5 %copy-start.11 = (bf16[40,2,640]{2,1,0:T(2,128)(2,1)S(1)}, bf16[40,2,640]{2,1,0:T(2,128)(2,1)}, u32[]{:S(2)}) copy-start(bf16[40,2,640]{2,1,0:T(2,128)(2,1)} %param.16) | copy-start | bytes 307204
  7.2 9.2 %copy-start.26 = (s32[8]{0:T(128)S(1)}, s32[8]{0:T(128)}, u32[]{:S(2)}) copy-start(s32[8]{0:T(128)} %param.22) | copy-start | bytes 100
  9.4 24.3 %copy-start.13 = (f32[2560]{0:T(1024)S(1)}, f32[2560]{0:T(1024)}, u32[]{:S(2)}) copy-start(f32[2560]{0:T(1024)} %param.17) | copy-start | bytes 30724
  9.4 23.8 %all-to-all-start = ((bf16[8,256,320]{1,2,0:T(8,128)(2,1)}), bf16[8,256,320]{1,2,0:T(8,128)(2,1)S(1)}, u32[]{:S(2)}, u32[]{:S(2)}) async-start(bf16[8,256,320]{1,2,0:T(8,128)(2,1)} %broadcast_in_dim.33), calls=%async_computation | async-start | bytes 2621440 | tf_op jit(solution)/shard_map/all_to_all | solution.py:35
  15.6 211.7 %all-gather.2.cloned.1.call-start = ((), (), s32[]{:S(2)}) async-start(), calls=%async_computation.4 | async-start | bytes 6656000 | tf_op jit(solution)/shard_map/all_gather | solution.py:169
  16.5 17.1 %copy-start.19 = (s32[8,1]{0,1:T(1,128)}, s32[8,1]{0,1:T(1,128)S(1)}, u32[]{:S(2)}) copy-start(s32[8,1]{0,1:T(1,128)S(1)} %reduce-window.8) | copy-start | bytes 100
  16.6 17.1 %copy-start.23 = (s32[256]{0:T(256)}, s32[256]{0:T(256)S(1)}, u32[]{:S(2)}) copy-start(s32[256]{0:T(256)S(1)} %iota_add_fusion.2) | copy-start | bytes 3076
  35.1 7.8 %copy-start.21 = (f32[256]{0:T(256)S(1)}, f32[256]{0:T(256)}, u32[]{:S(2)}) copy-start(f32[256]{0:T(256)} %param.21) | copy-start | bytes 3076
  35.8 7.0 %collective-permute-start = (bf16[256,256]{0,1:T(8,128)(2,1)S(1)}, bf16[256,256]{0,1:T(8,128)(2,1)S(1)}, u32[]{:S(2)}, u32[]{:S(2)}) collective-permute-start(bf16[256,256]{0,1:T(8,128)(2,1)S(1)} %convolution_convert_fusion), channel_id=1, source_target_pairs={{0,64},{64,0},{128,192},{192,128},{1,65},{65,1},{129,193},{193,129... | collective-permute-start | bytes 393224 | tf_op jit(solution)/shard_map/ppermute | solution.py:17
  44.3 10.8 %copy-start.6 = (bf16[256,128]{0,1:T(8,128)(2,1)}, bf16[256,128]{0,1:T(8,128)(2,1)S(1)}, u32[]{:S(2)}) copy-start(bf16[256,128]{0,1:T(8,128)(2,1)S(1)} %get-tuple-element.8) | copy-start | bytes 196612
  45.0 24.1 %collective-permute-start.2 = (bf16[2,256,256]{1,2,0:T(8,128)(2,1)}, bf16[2,256,256]{1,2,0:T(8,128)(2,1)S(1)}, u32[]{:S(2)}, u32[]{:S(2)}) collective-permute-start(bf16[2,256,256]{1,2,0:T(8,128)(2,1)} %get-tuple-element.16), channel_id=1, source_target_pairs={{0,4},{1,5},{2,6},{3,7},{4,8},{5,9},{6,10},{7,11},{8,12},{9,13},{1... | collective-permute-start | bytes 786440 | tf_op jit(solution)/shard_map/ppermute | solution.py:23
  55.0 20.6 %collective-permute-start.3 = (bf16[2,256,256]{1,2,0:T(8,128)(2,1)}, bf16[2,256,256]{1,2,0:T(8,128)(2,1)S(1)}, u32[]{:S(2)}, u32[]{:S(2)}) collective-permute-start(bf16[2,256,256]{1,2,0:T(8,128)(2,1)} %get-tuple-element.16), channel_id=1, source_target_pairs={{0,6},{1,7},{2,8},{3,9},{4,10},{5,11},{6,12},{7,13},{8,14},{9,15},... | collective-permute-start | bytes 786440 | tf_op jit(solution)/shard_map/ppermute | solution.py:23
  57.0 30.1 %collective-permute-start.1 = (bf16[2,256,256]{1,2,0:T(8,128)(2,1)}, bf16[2,256,256]{1,2,0:T(8,128)(2,1)}, u32[]{:S(2)}, u32[]{:S(2)}) collective-permute-start(bf16[2,256,256]{1,2,0:T(8,128)(2,1)} %get-tuple-element.16), channel_id=1, source_target_pairs={{0,2},{1,3},{2,4},{3,5},{4,6},{5,7},{6,8},{7,9},{8,10},{9,11},{10,... | collective-permute-start | bytes 786440 | tf_op jit(solution)/shard_map/ppermute | solution.py:23
  64.4 106.5 %all-to-all-start.2 = ((bf16[256,8,320]{0,2,1:T(8,128)(2,1)}), bf16[256,8,320]{0,2,1:T(8,128)(2,1)}, u32[]{:S(2)}, u32[]{:S(2)}) async-start(bf16[256,8,320]{0,2,1:T(8,128)(2,1)} %bitcast.73), calls=%async_computation.2 | async-start | bytes 2621440 | tf_op jit(solution)/shard_map/all_to_all | solution.py:91
  89.2 43.5 %collective-permute-start.4 = (bf16[4,2,256,256]{2,3,1,0:T(8,128)(2,1)}, bf16[4,2,256,256]{2,3,1,0:T(8,128)(2,1)}, u32[]{:S(2)}, u32[]{:S(2)}) collective-permute-start(bf16[4,2,256,256]{2,3,1,0:T(8,128)(2,1)} %pad_maximum_fusion), channel_id=1, source_target_pairs={{0,8},{1,9},{2,10},{3,11},{4,12},{5,13},{6,14},{7,15},{8,16},{9,17... | collective-permute-start | bytes 3145736 | tf_op jit(solution)/shard_map/ppermute | solution.py:23
  91.8 50.2 %copy-start.20 = (s32[9]{0:T(128)S(1)}, s32[9]{0:T(128)}, u32[]{:S(2)}) copy-start(s32[9]{0:T(128)} %get-tuple-element.31) | copy-start | bytes 112
  91.8 47.5 %collective-permute-start.5 = (bf16[2,256,256]{1,2,0:T(8,128)(2,1)}, bf16[2,256,256]{1,2,0:T(8,128)(2,1)S(1)}, u32[]{:S(2)}, u32[]{:S(2)}) collective-permute-start(bf16[2,256,256]{1,2,0:T(8,128)(2,1)} %get-tuple-element.16), channel_id=1, source_target_pairs={{0,16},{1,17},{2,18},{3,19},{4,20},{5,21},{6,22},{7,23},{8,24},{9,... | collective-permute-start | bytes 786440 | tf_op jit(solution)/shard_map/ppermute | solution.py:23
  135.0 9.9 %copy-start.22 = (f32[256]{0:T(256)S(1)}, f32[256]{0:T(256)}, u32[]{:S(2)}) copy-start(f32[256]{0:T(256)} %param.20) | copy-start | bytes 3076
  135.0 10.0 %copy-start.18 = (f32[128]{0:T(128)S(1)}, f32[128]{0:T(128)}, u32[]{:S(2)}) copy-start(f32[128]{0:T(128)} %copy-done.17) | copy-start | bytes 1540
  140.1 17.1 %collective-permute-start.6 = (bf16[9,2,256,256]{2,3,1,0:T(8,128)(2,1)}, bf16[9,2,256,256]{2,3,1,0:T(8,128)(2,1)}, u32[]{:S(2)}, u32[]{:S(2)}) collective-permute-start(bf16[9,2,256,256]{2,3,1,0:T(8,128)(2,1)} %bitcast_dynamic-update-slice_fusion), channel_id=1, source_target_pairs={{0,1},{1,0},{2,3},{3,2},{4,5},{5,4},{6,7},{7,6},{8,9},{9,8},{10,11... | collective-permute-start | bytes 7077896 | tf_op jit(solution)/shard_map/ppermute | solution.py:17
  199.3 20.9 %all-to-all-start.3 = ((bf16[8,256,320]{1,2,0:T(8,128)(2,1)}), bf16[8,256,320]{1,2,0:T(8,128)(2,1)}, u32[]{:S(2)}, u32[]{:S(2)}) async-start(bf16[8,256,320]{1,2,0:T(8,128)(2,1)} %broadcast_in_dim.41), calls=%async_computation.3 | async-start | bytes 2621440 | tf_op jit(solution)/shard_map/all_to_all | solution.py:35
  203.9 20.0 %copy-start.14 = (f32[2560]{0:T(1024)S(1)}, f32[2560]{0:T(1024)}, u32[]{:S(2)}) copy-start(f32[2560]{0:T(1024)} %param.19) | copy-start | bytes 30724
  204.6 22.7 %copy-start.7 = (bf16[2,128,256]{2,1,0:T(8,128)(2,1)}, bf16[2,128,256]{2,1,0:T(8,128)(2,1)S(1)}, u32[]{:S(2)}) copy-start(bf16[2,128,256]{2,1,0:T(8,128)(2,1)S(1)} %scatter_fusion) | copy-start | bytes 393220
  (15 other events, 54.7 us)
Sparse Core Ops, SparseCore 0:
  19.7 120.7 all-gather.1

commit v4 on v2

--- a/solution.py
+++ b/solution.py
@@ -126,8 +126,12 @@
     for step in range(1, near_blocks):
         near.append(shifted(key_block, "seq", 2 * step))
     series = jnp.stack(near)
-    received = shifted(series, "seq", 2 * near_blocks)
-    series = jnp.concatenate([series, received], axis=0)
+    slow = near_blocks // 2
+    early = [i for i in range(near_blocks) if i != slow]
+    received_early = shifted(jnp.stack([near[i] for i in early]), "seq", 2 * near_blocks)
+    received_late = shifted(near[slow], "seq", 2 * near_blocks)
+    far = [received_early[early.index(i)] if i != slow else received_late for i in range(near_blocks)]
+    series = jnp.concatenate([series, jnp.stack(far)], axis=0)
     series = jnp.concatenate([series, shifted(key_block, "seq", 2 * half_span)[None]], axis=0)
     partner = swapped(series, "seq", 0)
     parity = lax.axis_index("seq") % 2

time: 236 us -> 246 us (1.042)
  the two profiles are of different devices: /device:TPU:168 before, /device:TPU:480 now
where the time goes in v4:
time: 246 us; the launch traced here: 245 us
  waiting for transfers between devices  127 us (52%)
  starting transfers between devices  47.6 us (19%)
  local copies, waits for them, and re-layouts  32.9 us (13%)
  matrix products  15.1 us (6%)
  between operations  14.5 us (6%)
  other arithmetic  8.09 us (3%)
    ppermute x6, waiting for transfers between devices, shifted(): return lax.ppermute(block, axis, route)  67.5 us
    all_to_all x4, waiting for transfers between devices, group_parts(): return lax.all_to_all(spread, GROUP, 0, 0, tiled=True)  46.5 us
    all_to_all x4, starting transfers between devices, group_parts(): return lax.all_to_all(spread, GROUP, 0, 0, tiled=True)  20.3 us
    ppermute x6, starting transfers between devices, shifted(): return lax.ppermute(block, axis, route)  17.3 us
    ppermute x2, waiting for transfers between devices, swapped(): return lax.ppermute(value, axis, pairs)  12.8 us
    unnamed x56, local copies, waits for them, and re-layouts  11.3 us
    slice x3, local copies, waits for them, and re-layouts, part_scores(): keys = stack[:, 0].reshape(-1, head_width)  7.69 us
    dot_general x2, matrix products, part_scores(): lax.dot_general(queries, keys, (((1,), (1,)), ((), ())), preferred_elemen...  5.97 us
  transfers between devices with their start and end apart: 14, of which 9 were waited for; matrix products, arithmetic and copies ran while one was open for 19% of the time, Pallas kernels for 0%

profile of v4, /device:TPU:480, one launch (start us, length us, event | category | flops | bytes accessed | tf_op | source)
XLA Modules:
  0.0 245.1 jit_solution(11170195874669512795)
XLA Ops:
  9.4 5.9 %all-to-all-start = ((bf16[8,256,320]{1,2,0:T(8,128)(2,1)}), bf16[8,256,320]{1,2,0:T(8,128)(2,1)S(1)}, u32[]{:S(2)}, u32[]{:S(2)}) async-start(bf16[8,256,320]{1,2,0:T(8,128)(2,1)} %broadcast_in_dim.36), calls=%async_computation | async-start | bytes 2621440 | tf_op jit(solution)/shard_map/all_to_all | solution.py:35
  16.0 2.4 copy.34
  19.3 13.0 %all-to-all-done = bf16[8,256,320]{1,2,0:T(8,128)(2,1)S(1)} async-done(((bf16[8,256,320]{1,2,0:T(8,128)(2,1)}), bf16[8,256,320]{1,2,0:T(8,128)(2,1)S(1)}, u32[]{:S(2)}, u32[]{:S(2)}) %all-to-all-start) | async-done | bytes 1310752 | tf_op jit(solution)/shard_map/all_to_all | solution.py:35
  32.3 4.7 %all-to-all-start.2 = ((bf16[256,8,320]{0,2,1:T(8,128)(2,1)}), bf16[256,8,320]{0,2,1:T(8,128)(2,1)}, u32[]{:S(2)}, u32[]{:S(2)}) async-start(bf16[256,8,320]{0,2,1:T(8,128)(2,1)} %bitcast.72), calls=%async_computation.2 | async-start | bytes 2621440 | tf_op jit(solution)/shard_map/all_to_all | solution.py:95
  39.6 3.4 %collective-permute-start = (bf16[256,256]{0,1:T(8,128)(2,1)S(1)}, bf16[256,256]{0,1:T(8,128)(2,1)S(1)}, u32[]{:S(2)}, u32[]{:S(2)}) collective-permute-start(bf16[256,256]{0,1:T(8,128)(2,1)S(1)} %convolution_convert_fusion), channel_id=1, source_target_pairs={{0,64},{64,0},{128,192},{192,128},{1,65},{65,1},{129,193},{193,129... | collective-permute-start | bytes 393224 | tf_op jit(solution)/shard_map/ppermute | solution.py:17
  43.0 12.8 %collective-permute-done = bf16[256,256]{0,1:T(8,128)(2,1)S(1)} collective-permute-done((bf16[256,256]{0,1:T(8,128)(2,1)S(1)}, bf16[256,256]{0,1:T(8,128)(2,1)S(1)}, u32[]{:S(2)}, u32[]{:S(2)}) %collective-permute-start) | collective-permute-done | bytes 131104 | tf_op jit(solution)/shard_map/ppermute | solution.py:17
  58.0 2.6 %collective-permute-start.3 = (bf16[2,256,256]{1,2,0:T(8,128)(2,1)}, bf16[2,256,256]{1,2,0:T(8,128)(2,1)S(1)}, u32[]{:S(2)}, u32[]{:S(2)}) collective-permute-start(bf16[2,256,256]{1,2,0:T(8,128)(2,1)} %get-tuple-element.20), channel_id=1, source_target_pairs={{0,6},{1,7},{2,8},{3,9},{4,10},{5,11},{6,12},{7,13},{8,14},{9,15},... | collective-permute-start | bytes 786440 | tf_op jit(solution)/shard_map/ppermute | solution.py:23
  60.6 5.5 %collective-permute-start.1 = (bf16[2,256,256]{1,2,0:T(8,128)(2,1)}, bf16[2,256,256]{1,2,0:T(8,128)(2,1)S(1)}, u32[]{:S(2)}, u32[]{:S(2)}) collective-permute-start(bf16[2,256,256]{1,2,0:T(8,128)(2,1)} %get-tuple-element.20), channel_id=1, source_target_pairs={{0,2},{1,3},{2,4},{3,5},{4,6},{5,7},{6,8},{7,9},{8,10},{9,11},{10,... | collective-permute-start | bytes 786440 | tf_op jit(solution)/shard_map/ppermute | solution.py:23
  68.6 2.7 %collective-permute-start.6 = (bf16[2,256,256]{1,2,0:T(8,128)(2,1)}, bf16[2,256,256]{1,2,0:T(8,128)(2,1)S(1)}, u32[]{:S(2)}, u32[]{:S(2)}) collective-permute-start(bf16[2,256,256]{1,2,0:T(8,128)(2,1)} %get-tuple-element.20), channel_id=1, source_target_pairs={{0,16},{1,17},{2,18},{3,19},{4,20},{5,21},{6,22},{7,23},{8,24},{9,... | collective-permute-start | bytes 786440 | tf_op jit(solution)/shard_map/ppermute | solution.py:23
  72.9 36.1 %collective-permute-done.1 = bf16[2,256,256]{1,2,0:T(8,128)(2,1)S(1)} collective-permute-done((bf16[2,256,256]{1,2,0:T(8,128)(2,1)}, bf16[2,256,256]{1,2,0:T(8,128)(2,1)S(1)}, u32[]{:S(2)}, u32[]{:S(2)}) %collective-permute-start.1) | collective-permute-done | bytes 262176 | tf_op jit(solution)/shard_map/ppermute | solution.py:23
  109.1 2.7 %collective-permute-start.4 = (bf16[3,2,256,256]{2,3,1,0:T(8,128)(2,1)S(1)}, bf16[3,2,256,256]{2,3,1,0:T(8,128)(2,1)S(1)}, u32[]{:S(2)}, u32[]{:S(2)}) collective-permute-start(bf16[3,2,256,256]{2,3,1,0:T(8,128)(2,1)S(1)} %pad_maximum_fusion), channel_id=1, source_target_pairs={{0,8},{1,9},{2,10},{3,11},{4,12},{5,13},{6,14},{7,15},{8,16},{9,17... | collective-permute-start | bytes 2359304 | tf_op jit(solution)/shard_map/ppermute | solution.py:23
  117.5 25.4 %collective-permute-done.4 = bf16[3,2,256,256]{2,3,1,0:T(8,128)(2,1)S(1)} collective-permute-done((bf16[3,2,256,256]{2,3,1,0:T(8,128)(2,1)S(1)}, bf16[3,2,256,256]{2,3,1,0:T(8,128)(2,1)S(1)}, u32[]{:S(2)}, u32[]{:S(2)}) %collective-permute-start.4) | collective-permute-done | bytes 786464 | tf_op jit(solution)/shard_map/ppermute | solution.py:23
  143.7 4.5 %collective-permute-done.5 = bf16[2,256,256]{1,2,0:T(8,128)(2,1)S(1)} collective-permute-done((bf16[2,256,256]{1,2,0:T(8,128)(2,1)}, bf16[2,256,256]{1,2,0:T(8,128)(2,1)S(1)}, u32[]{:S(2)}, u32[]{:S(2)}) %collective-permute-start.5) | collective-permute-done | bytes 262176 | tf_op jit(solution)/shard_map/ppermute | solution.py:23
  154.5 2.8 %fusion.57 = (bf16[9,1,256,256]{2,3,1,0:T(8,128)(2,1)}, bf16[9,1,256,256]{2,3,1,0:T(8,128)(2,1)S(1)}) fusion(bf16[9,2,256,256]{2,3,1,0:T(8,128)(2,1)} %bitcast_dynamic-update-slice_fusion), kind=kLoop, calls=%fused_computation.114 | loop fusion | bytes 4718592 | tf_op jit(solution)/shard_map/slice | solution.py:150
  161.3 3.6 %fusion.61 = (f32[256]{0:T(256)S(1)}, f32[256,2304]{1,0:T(8,128)}) fusion(bf16[2304,256]{1,0:T(8,128)(2,1)} %bitcast.76, bf16[256,128]{0,1:T(8,128)(2,1)S(1)} %get-tuple-element.18, bf16[256,128]{0,1:T(8,128)(2,1)S(1)} %get-tuple-element.17, s32[256]{0:T(256)S(1)} %copy-done.20, s32[2304]{0:T(1024)S(1)} %add.186, s32[256]{0:T(256)S(1)} %copy-done.12, ...), kind=kOutput, calls=%fused_computation.118 | convolution fusion | flops 305790720 | bytes 3691520 | tf_op jit(solution)/shard_map/dot_general | solution.py:151
  164.9 2.8 %fusion.56 = (bf16[9,1,256,256]{2,3,1,0:T(8,128)(2,1)S(1)}, bf16[9,1,256,256]{2,3,1,0:T(8,128)(2,1)}) fusion(bf16[9,2,256,256]{2,3,1,0:T(8,128)(2,1)} %collective-permute-done.7), kind=kLoop, calls=%fused_computation.113 | loop fusion | bytes 4718592 | tf_op jit(solution)/shard_map/slice | solution.py:169
  167.7 2.4 copy.31
  178.3 5.4 %all-to-all-start.1 = ((bf16[8,256,256]{2,1,0:T(8,128)(2,1)}), bf16[8,256,256]{2,1,0:T(8,128)(2,1)S(1)}, u32[]{:S(2)}, u32[]{:S(2)}) async-start(bf16[8,256,256]{2,1,0:T(8,128)(2,1)} %broadcast_in_dim.42), calls=%async_computation.1 | async-start | bytes 2097152 | tf_op jit(solution)/shard_map/all_to_all | solution.py:35
  184.4 14.1 %all-to-all-done.1 = bf16[8,256,256]{2,1,0:T(8,128)(2,1)S(1)} async-done(((bf16[8,256,256]{2,1,0:T(8,128)(2,1)}), bf16[8,256,256]{2,1,0:T(8,128)(2,1)S(1)}, u32[]{:S(2)}, u32[]{:S(2)}) %all-to-all-start.1) | async-done | bytes 1048608 | tf_op jit(solution)/shard_map/all_to_all | solution.py:35
  201.1 4.2 %all-to-all-start.3 = ((f32[8,4,256]{2,1,0:T(4,128)}), f32[8,4,256]{2,1,0:T(4,128)S(1)}, u32[]{:S(2)}, u32[]{:S(2)}) async-start(f32[8,4,256]{2,1,0:T(4,128)} %broadcast_in_dim.43), calls=%async_computation.3 | async-start | bytes 65536 | tf_op jit(solution)/shard_map/all_to_all | solution.py:35
  206.1 4.1 %all-to-all-done.3 = f32[8,4,256]{2,1,0:T(4,128)S(1)} async-done(((f32[8,4,256]{2,1,0:T(4,128)}), f32[8,4,256]{2,1,0:T(4,128)S(1)}, u32[]{:S(2)}, u32[]{:S(2)}) %all-to-all-start.3) | async-done | bytes 32800 | tf_op jit(solution)/shard_map/all_to_all | solution.py:35
  211.5 4.9 %all-to-all-start.4 = ((bf16[8,256,320]{1,2,0:T(8,128)(2,1)}), bf16[8,256,320]{1,2,0:T(8,128)(2,1)S(1)}, u32[]{:S(2)}, u32[]{:S(2)}) async-start(bf16[8,256,320]{1,2,0:T(8,128)(2,1)} %broadcast_in_dim.44), calls=%async_computation.4 | async-start | bytes 2621440 | tf_op jit(solution)/shard_map/all_to_all | solution.py:35
  217.2 15.3 %all-to-all-done.4 = bf16[8,256,320]{1,2,0:T(8,128)(2,1)S(1)} async-done(((bf16[8,256,320]{1,2,0:T(8,128)(2,1)}), bf16[8,256,320]{1,2,0:T(8,128)(2,1)S(1)}, u32[]{:S(2)}, u32[]{:S(2)}) %all-to-all-start.4) | async-done | bytes 1310752 | tf_op jit(solution)/shard_map/all_to_all | solution.py:35
  232.6 4.8 %fusion.63 = f32[256,1280]{1,0:T(8,128)S(1)} fusion(bf16[256,2560]{0,1:T(8,128)(2,1)S(1)} %bitcast.71, bf16[2560,1280]{1,0:T(8,128)(2,1)} %all-gather.2.cloned.1.call-done), kind=kOutput, calls=%fused_computation.120 | convolution fusion | flops 1677721600 | bytes 9175040 | tf_op jit(solution)/shard_map/dot_general | solution.py:203
  (128 shorter events, 44.6 us)
Async XLA Ops:
  7.2 146.0 %copy-start = (bf16[2560,256]{1,0:T(8,128)(2,1)S(1)}, bf16[2560,256]{1,0:T(8,128)(2,1)}, u32[]{:S(2)}) copy-start(bf16[2560,256]{1,0:T(8,128)(2,1)} %param.13) | copy-start | bytes 3932164
  9.4 22.9 %all-to-all-start = ((bf16[8,256,320]{1,2,0:T(8,128)(2,1)}), bf16[8,256,320]{1,2,0:T(8,128)(2,1)S(1)}, u32[]{:S(2)}, u32[]{:S(2)}) async-start(bf16[8,256,320]{1,2,0:T(8,128)(2,1)} %broadcast_in_dim.36), calls=%async_computation | async-start | bytes 2621440 | tf_op jit(solution)/shard_map/all_to_all | solution.py:35
  15.2 217.3 %all-gather.2.cloned.1.call-start = ((), (), s32[]{:S(2)}) async-start(), calls=%async_computation.5 | async-start | bytes 6656000 | tf_op jit(solution)/shard_map/all_gather | solution.py:200
  18.4 19.0 %copy-start.10 = (f32[2560]{0:T(1024)S(1)}, f32[2560]{0:T(1024)}, u32[]{:S(2)}) copy-start(f32[2560]{0:T(1024)} %param.17) | copy-start | bytes 30724
  18.6 13.7 %copy-start.15 = (s32[8,1]{0,1:T(1,128)}, s32[8,1]{0,1:T(1,128)S(1)}, u32[]{:S(2)}) copy-start(s32[8,1]{0,1:T(1,128)S(1)} %reduce-window.8) | copy-start | bytes 100
  32.3 145.0 %all-to-all-start.2 = ((bf16[256,8,320]{0,2,1:T(8,128)(2,1)}), bf16[256,8,320]{0,2,1:T(8,128)(2,1)}, u32[]{:S(2)}, u32[]{:S(2)}) async-start(bf16[256,8,320]{0,2,1:T(8,128)(2,1)} %bitcast.72), calls=%async_computation.2 | async-start | bytes 2621440 | tf_op jit(solution)/shard_map/all_to_all | solution.py:95
  38.9 17.0 %copy-start.17 = (f32[256]{0:T(256)S(1)}, f32[256]{0:T(256)}, u32[]{:S(2)}) copy-start(f32[256]{0:T(256)} %param.21) | copy-start | bytes 3076
  39.6 16.3 %collective-permute-start = (bf16[256,256]{0,1:T(8,128)(2,1)S(1)}, bf16[256,256]{0,1:T(8,128)(2,1)S(1)}, u32[]{:S(2)}, u32[]{:S(2)}) collective-permute-start(bf16[256,256]{0,1:T(8,128)(2,1)S(1)} %convolution_convert_fusion), channel_id=1, source_target_pairs={{0,64},{64,0},{128,192},{192,128},{1,65},{65,1},{129,193},{193,129... | collective-permute-start | bytes 393224 | tf_op jit(solution)/shard_map/ppermute | solution.py:17
  43.0 25.5 %copy-start.13 = (f32[128]{0:T(128)}, f32[128]{0:T(128)S(1)}, u32[]{:S(2)}) copy-start(f32[128]{0:T(128)S(1)} %negate_power_fusion) | copy-start | bytes 1540
  58.0 14.9 %collective-permute-start.3 = (bf16[2,256,256]{1,2,0:T(8,128)(2,1)}, bf16[2,256,256]{1,2,0:T(8,128)(2,1)S(1)}, u32[]{:S(2)}, u32[]{:S(2)}) collective-permute-start(bf16[2,256,256]{1,2,0:T(8,128)(2,1)} %get-tuple-element.20), channel_id=1, source_target_pairs={{0,6},{1,7},{2,8},{3,9},{4,10},{5,11},{6,12},{7,13},{8,14},{9,15},... | collective-permute-start | bytes 786440 | tf_op jit(solution)/shard_map/ppermute | solution.py:23
  60.6 48.3 %collective-permute-start.1 = (bf16[2,256,256]{1,2,0:T(8,128)(2,1)}, bf16[2,256,256]{1,2,0:T(8,128)(2,1)S(1)}, u32[]{:S(2)}, u32[]{:S(2)}) collective-permute-start(bf16[2,256,256]{1,2,0:T(8,128)(2,1)} %get-tuple-element.20), channel_id=1, source_target_pairs={{0,2},{1,3},{2,4},{3,5},{4,6},{5,7},{6,8},{7,9},{8,10},{9,11},{10,... | collective-permute-start | bytes 786440 | tf_op jit(solution)/shard_map/ppermute | solution.py:23
  66.6 45.9 %collective-permute-start.2 = (bf16[2,256,256]{1,2,0:T(8,128)(2,1)}, bf16[2,256,256]{1,2,0:T(8,128)(2,1)}, u32[]{:S(2)}, u32[]{:S(2)}) collective-permute-start(bf16[2,256,256]{1,2,0:T(8,128)(2,1)} %get-tuple-element.20), channel_id=1, source_target_pairs={{0,4},{1,5},{2,6},{3,7},{4,8},{5,9},{6,10},{7,11},{8,12},{9,13},{1... | collective-permute-start | bytes 786440 | tf_op jit(solution)/shard_map/ppermute | solution.py:23
  68.6 81.1 %collective-permute-start.6 = (bf16[2,256,256]{1,2,0:T(8,128)(2,1)}, bf16[2,256,256]{1,2,0:T(8,128)(2,1)S(1)}, u32[]{:S(2)}, u32[]{:S(2)}) collective-permute-start(bf16[2,256,256]{1,2,0:T(8,128)(2,1)} %get-tuple-element.20), channel_id=1, source_target_pairs={{0,16},{1,17},{2,18},{3,19},{4,20},{5,21},{6,22},{7,23},{8,24},{9,... | collective-permute-start | bytes 786440 | tf_op jit(solution)/shard_map/ppermute | solution.py:23
  109.0 43.3 %copy-start.16 = (s32[9]{0:T(128)S(1)}, s32[9]{0:T(128)}, u32[]{:S(2)}) copy-start(s32[9]{0:T(128)} %get-tuple-element.40) | copy-start | bytes 112
  109.1 44.1 %copy-start.3 = (bf16[256,2560]{0,1:T(8,128)(2,1)S(1)}, bf16[256,2560]{0,1:T(8,128)(2,1)}, u32[]{:S(2)}) copy-start(bf16[256,2560]{0,1:T(8,128)(2,1)} %copy-done.2) | copy-start | bytes 3932164
  109.1 33.8 %collective-permute-start.4 = (bf16[3,2,256,256]{2,3,1,0:T(8,128)(2,1)S(1)}, bf16[3,2,256,256]{2,3,1,0:T(8,128)(2,1)S(1)}, u32[]{:S(2)}, u32[]{:S(2)}) collective-permute-start(bf16[3,2,256,256]{2,3,1,0:T(8,128)(2,1)S(1)} %pad_maximum_fusion), channel_id=1, source_target_pairs={{0,8},{1,9},{2,10},{3,11},{4,12},{5,13},{6,14},{7,15},{8,16},{9,17... | collective-permute-start | bytes 2359304 | tf_op jit(solution)/shard_map/ppermute | solution.py:23
  112.5 35.7 %collective-permute-start.5 = (bf16[2,256,256]{1,2,0:T(8,128)(2,1)}, bf16[2,256,256]{1,2,0:T(8,128)(2,1)S(1)}, u32[]{:S(2)}, u32[]{:S(2)}) collective-permute-start(bf16[2,256,256]{1,2,0:T(8,128)(2,1)} %collective-permute-done.2), channel_id=1, source_target_pairs={{0,8},{1,9},{2,10},{3,11},{4,12},{5,13},{6,14},{7,15},{8,16},{9,17... | collective-permute-start | bytes 786440 | tf_op jit(solution)/shard_map/ppermute | solution.py:23
  143.7 10.1 %copy-start.18 = (f32[256]{0:T(256)S(1)}, f32[256]{0:T(256)}, u32[]{:S(2)}) copy-start(f32[256]{0:T(256)} %param.20) | copy-start | bytes 3076
  150.4 14.5 %collective-permute-start.7 = (bf16[9,2,256,256]{2,3,1,0:T(8,128)(2,1)}, bf16[9,2,256,256]{2,3,1,0:T(8,128)(2,1)}, u32[]{:S(2)}, u32[]{:S(2)}) collective-permute-start(bf16[9,2,256,256]{2,3,1,0:T(8,128)(2,1)} %bitcast_dynamic-update-slice_fusion), channel_id=1, source_target_pairs={{0,1},{1,0},{2,3},{3,2},{4,5},{5,4},{6,7},{7,6},{8,9},{9,8},{10,11... | collective-permute-start | bytes 7077896 | tf_op jit(solution)/shard_map/ppermute | solution.py:17
  177.3 21.3 %copy-start.6 = (bf16[256,320]{0,1:T(8,128)(2,1)S(1)}, bf16[256,320]{0,1:T(8,128)(2,1)}, u32[]{:S(2)}) copy-start(bf16[256,320]{0,1:T(8,128)(2,1)} %param.12) | copy-start | bytes 491524
  178.3 20.3 %all-to-all-start.1 = ((bf16[8,256,256]{2,1,0:T(8,128)(2,1)}), bf16[8,256,256]{2,1,0:T(8,128)(2,1)S(1)}, u32[]{:S(2)}, u32[]{:S(2)}) async-start(bf16[8,256,256]{2,1,0:T(8,128)(2,1)} %broadcast_in_dim.42), calls=%async_computation.1 | async-start | bytes 2097152 | tf_op jit(solution)/shard_map/all_to_all | solution.py:35
  201.1 9.0 %all-to-all-start.3 = ((f32[8,4,256]{2,1,0:T(4,128)}), f32[8,4,256]{2,1,0:T(4,128)S(1)}, u32[]{:S(2)}, u32[]{:S(2)}) async-start(f32[8,4,256]{2,1,0:T(4,128)} %broadcast_in_dim.43), calls=%async_computation.3 | async-start | bytes 65536 | tf_op jit(solution)/shard_map/all_to_all | solution.py:35
  211.5 21.1 %all-to-all-start.4 = ((bf16[8,256,320]{1,2,0:T(8,128)(2,1)}), bf16[8,256,320]{1,2,0:T(8,128)(2,1)S(1)}, u32[]{:S(2)}, u32[]{:S(2)}) async-start(bf16[8,256,320]{1,2,0:T(8,128)(2,1)} %broadcast_in_dim.44), calls=%async_computation.4 | async-start | bytes 2621440 | tf_op jit(solution)/shard_map/all_to_all | solution.py:35
  217.2 20.1 %copy-start.7 = (bf16[2,128,256]{2,1,0:T(8,128)(2,1)}, bf16[2,128,256]{2,1,0:T(8,128)(2,1)S(1)}, u32[]{:S(2)}) copy-start(bf16[2,128,256]{2,1,0:T(8,128)(2,1)S(1)} %scatter_fusion) | copy-start | bytes 393220
  (14 other events, 51.6 us)
Sparse Core Ops, SparseCore 0:
  19.3 116.1 all-gather.1

commit v5 on v4

--- a/solution.py
+++ b/solution.py
@@ -127,10 +127,13 @@
         near.append(shifted(key_block, "seq", 2 * step))
     series = jnp.stack(near)
     slow = near_blocks // 2
-    early = [i for i in range(near_blocks) if i != slow]
+    early = [i for i in range(1, near_blocks) if i != slow]
+    received_own = shifted(near[0], "seq", 2 * near_blocks)
     received_early = shifted(jnp.stack([near[i] for i in early]), "seq", 2 * near_blocks)
     received_late = shifted(near[slow], "seq", 2 * near_blocks)
-    far = [received_early[early.index(i)] if i != slow else received_late for i in range(near_blocks)]
+    far = [received_own] + [
+        received_early[early.index(i)] if i != slow else received_late for i in range(1, near_blocks)
+    ]
     series = jnp.concatenate([series, jnp.stack(far)], axis=0)
     series = jnp.concatenate([series, shifted(key_block, "seq", 2 * half_span)[None]], axis=0)
     partner = swapped(series, "seq", 0)

time: 246 us -> 239 us (0.972)
  the two profiles are of different devices: /device:TPU:480 before, /device:TPU:496 now
where the time goes in v5:
time: 239 us; the launch traced here: 238 us
  waiting for transfers between devices  119 us (50%)
  starting transfers between devices  47.9 us (20%)
  local copies, waits for them, and re-layouts  33.8 us (14%)
  matrix products  15.1 us (6%)
  between operations  14.5 us (6%)
  other arithmetic  7.33 us (3%)
    ppermute x7, waiting for transfers between devices, shifted(): return lax.ppermute(block, axis, route)  60.5 us
    all_to_all x4, waiting for transfers between devices, group_parts(): return lax.all_to_all(spread, GROUP, 0, 0, tiled=True)  46.2 us
    all_to_all x4, starting transfers between devices, group_parts(): return lax.all_to_all(spread, GROUP, 0, 0, tiled=True)  20.1 us
    ppermute x7, starting transfers between devices, shifted(): return lax.ppermute(block, axis, route)  17.7 us
    ppermute x2, waiting for transfers between devices, swapped(): return lax.ppermute(value, axis, pairs)  12.4 us
    unnamed x57, local copies, waits for them, and re-layouts  12.2 us
    slice x3, local copies, waits for them, and re-layouts, part_scores(): keys = stack[:, 0].reshape(-1, head_width)  7.69 us
    dot_general x2, matrix products, part_scores(): lax.dot_general(queries, keys, (((1,), (1,)), ((), ())), preferred_elemen...  5.97 us
  transfers between devices with their start and end apart: 15, of which 8 were waited for; matrix products, arithmetic and copies ran while one was open for 19% of the time, Pallas kernels for 0%

profile of v5, /device:TPU:496, one launch (start us, length us, event | category | flops | bytes accessed | tf_op | source)
XLA Modules:
  0.0 237.8 jit_solution(10725854044629619404)
XLA Ops:
  9.4 5.9 %all-to-all-start = ((bf16[8,256,320]{1,2,0:T(8,128)(2,1)}), bf16[8,256,320]{1,2,0:T(8,128)(2,1)S(1)}, u32[]{:S(2)}, u32[]{:S(2)}) async-start(bf16[8,256,320]{1,2,0:T(8,128)(2,1)} %broadcast_in_dim.36), calls=%async_computation | async-start | bytes 2621440 | tf_op jit(solution)/shard_map/all_to_all | solution.py:35
  16.0 2.4 %copy.34 = bf16[256,2560]{0,1:T(8,128)(2,1)} copy(bf16[256,2560]{1,0:T(8,128)(2,1)} %param.15) | data formatting | bytes 2621440 | tf_op args[3]
  19.6 12.7 %all-to-all-done = bf16[8,256,320]{1,2,0:T(8,128)(2,1)S(1)} async-done(((bf16[8,256,320]{1,2,0:T(8,128)(2,1)}), bf16[8,256,320]{1,2,0:T(8,128)(2,1)S(1)}, u32[]{:S(2)}, u32[]{:S(2)}) %all-to-all-start) | async-done | bytes 1310752 | tf_op jit(solution)/shard_map/all_to_all | solution.py:35
  32.3 4.7 %all-to-all-start.2 = ((bf16[256,8,320]{0,2,1:T(8,128)(2,1)}), bf16[256,8,320]{0,2,1:T(8,128)(2,1)}, u32[]{:S(2)}, u32[]{:S(2)}) async-start(bf16[256,8,320]{0,2,1:T(8,128)(2,1)} %bitcast.73), calls=%async_computation.2 | async-start | bytes 2621440 | tf_op jit(solution)/shard_map/all_to_all | solution.py:95
  39.6 3.4 %collective-permute-start = (bf16[256,256]{0,1:T(8,128)(2,1)S(1)}, bf16[256,256]{0,1:T(8,128)(2,1)S(1)}, u32[]{:S(2)}, u32[]{:S(2)}) collective-permute-start(bf16[256,256]{0,1:T(8,128)(2,1)S(1)} %convolution_convert_fusion), channel_id=1, source_target_pairs={{0,64},{64,0},{128,192},{192,128},{1,65},{65,1},{129,193},{193,129... | collective-permute-start | bytes 393224 | tf_op jit(solution)/shard_map/ppermute | solution.py:17
  43.5 12.4 %collective-permute-done = bf16[256,256]{0,1:T(8,128)(2,1)S(1)} collective-permute-done((bf16[256,256]{0,1:T(8,128)(2,1)S(1)}, bf16[256,256]{0,1:T(8,128)(2,1)S(1)}, u32[]{:S(2)}, u32[]{:S(2)}) %collective-permute-start) | collective-permute-done | bytes 131104 | tf_op jit(solution)/shard_map/ppermute | solution.py:17
  59.3 6.1 %collective-permute-start.2 = (bf16[2,256,256]{1,2,0:T(8,128)(2,1)S(1)}, bf16[2,256,256]{1,2,0:T(8,128)(2,1)}, u32[]{:S(2)}, u32[]{:S(2)}) collective-permute-start(bf16[2,256,256]{1,2,0:T(8,128)(2,1)S(1)} %pad_maximum_fusion.1), channel_id=1, source_target_pairs={{0,4},{1,5},{2,6},{3,7},{4,8},{5,9},{6,10},{7,11},{8,12},{9,13},{1... | collective-permute-start | bytes 786440 | tf_op jit(solution)/shard_map/ppermute | solution.py:23
  71.3 33.9 %collective-permute-done.1 = bf16[2,256,256]{1,2,0:T(8,128)(2,1)S(1)} collective-permute-done((bf16[2,256,256]{1,2,0:T(8,128)(2,1)S(1)}, bf16[2,256,256]{1,2,0:T(8,128)(2,1)S(1)}, u32[]{:S(2)}, u32[]{:S(2)}) %collective-permute-start.1) | collective-permute-done | bytes 262176 | tf_op jit(solution)/shard_map/ppermute | solution.py:23
  105.3 2.7 %collective-permute-start.5 = (bf16[2,2,256,256]{2,3,1,0:T(8,128)(2,1)S(1)}, bf16[2,2,256,256]{2,3,1,0:T(8,128)(2,1)S(1)}, u32[]{:S(2)}, u32[]{:S(2)}) collective-permute-start(bf16[2,2,256,256]{2,3,1,0:T(8,128)(2,1)S(1)} %pad_maximum_fusion), channel_id=1, source_target_pairs={{0,8},{1,9},{2,10},{3,11},{4,12},{5,13},{6,14},{7,15},{8,16},{9,17... | collective-permute-start | bytes 1572872 | tf_op jit(solution)/shard_map/ppermute | solution.py:23
  113.7 22.0 %collective-permute-done.5 = bf16[2,2,256,256]{2,3,1,0:T(8,128)(2,1)S(1)} collective-permute-done((bf16[2,2,256,256]{2,3,1,0:T(8,128)(2,1)S(1)}, bf16[2,2,256,256]{2,3,1,0:T(8,128)(2,1)S(1)}, u32[]{:S(2)}, u32[]{:S(2)}) %collective-permute-start.5) | collective-permute-done | bytes 524320 | tf_op jit(solution)/shard_map/ppermute | solution.py:23
  136.4 4.7 %collective-permute-done.6 = bf16[2,256,256]{1,2,0:T(8,128)(2,1)S(1)} collective-permute-done((bf16[2,256,256]{1,2,0:T(8,128)(2,1)}, bf16[2,256,256]{1,2,0:T(8,128)(2,1)S(1)}, u32[]{:S(2)}, u32[]{:S(2)}) %collective-permute-start.6) | collective-permute-done | bytes 262176 | tf_op jit(solution)/shard_map/ppermute | solution.py:23
  147.4 2.8 %fusion.56 = (bf16[9,1,256,256]{2,3,1,0:T(8,128)(2,1)}, bf16[9,1,256,256]{2,3,1,0:T(8,128)(2,1)S(1)}) fusion(bf16[9,2,256,256]{2,3,1,0:T(8,128)(2,1)} %bitcast_dynamic-update-slice_fusion), kind=kLoop, calls=%fused_computation.114 | loop fusion | bytes 4718592 | tf_op jit(solution)/shard_map/slice | solution.py:153
  150.3 2.4 %copy.30 = bf16[9,1,256,256]{3,2,0,1:T(8,128)(2,1)} copy(bf16[9,1,256,256]{2,3,1,0:T(8,128)(2,1)} %get-tuple-element.15) | data formatting | bytes 2359296 | tf_op jit(solution)/shard_map/slice | solution.py:153
  154.2 3.6 %fusion.60 = (f32[256]{0:T(256)S(1)}, f32[256,2304]{1,0:T(8,128)}) fusion(bf16[2304,256]{1,0:T(8,128)(2,1)} %bitcast.77, bf16[256,128]{0,1:T(8,128)(2,1)S(1)} %get-tuple-element.18, bf16[256,128]{0,1:T(8,128)(2,1)S(1)} %get-tuple-element.17, s32[256]{0:T(256)S(1)} %copy-done.20, s32[2304]{0:T(1024)S(1)} %add.186, s32[256]{0:T(256)S(1)} %copy-done.12, ...), kind=kOutput, calls=%fused_computation.118 | convolution fusion | flops 305790720 | bytes 3691520 | tf_op jit(solution)/shard_map/dot_general | solution.py:154
  157.8 2.8 %fusion.55 = (bf16[9,1,256,256]{2,3,1,0:T(8,128)(2,1)S(1)}, bf16[9,1,256,256]{2,3,1,0:T(8,128)(2,1)}) fusion(bf16[9,2,256,256]{2,3,1,0:T(8,128)(2,1)} %collective-permute-done.8), kind=kLoop, calls=%fused_computation.113 | loop fusion | bytes 4718592 | tf_op jit(solution)/shard_map/slice | solution.py:172
  160.7 2.4 %copy.31 = bf16[9,1,256,256]{3,2,0,1:T(8,128)(2,1)} copy(bf16[9,1,256,256]{2,3,1,0:T(8,128)(2,1)} %get-tuple-element.14) | data formatting | bytes 2359296 | tf_op jit(solution)/shard_map/slice | solution.py:153
  164.6 2.4 fusion.61
  171.2 5.2 %all-to-all-start.1 = ((bf16[8,256,256]{2,1,0:T(8,128)(2,1)}), bf16[8,256,256]{2,1,0:T(8,128)(2,1)S(1)}, u32[]{:S(2)}, u32[]{:S(2)}) async-start(bf16[8,256,256]{2,1,0:T(8,128)(2,1)} %broadcast_in_dim.42), calls=%async_computation.1 | async-start | bytes 2097152 | tf_op jit(solution)/shard_map/all_to_all | solution.py:35
  177.2 14.1 %all-to-all-done.1 = bf16[8,256,256]{2,1,0:T(8,128)(2,1)S(1)} async-done(((bf16[8,256,256]{2,1,0:T(8,128)(2,1)}), bf16[8,256,256]{2,1,0:T(8,128)(2,1)S(1)}, u32[]{:S(2)}, u32[]{:S(2)}) %all-to-all-start.1) | async-done | bytes 1048608 | tf_op jit(solution)/shard_map/all_to_all | solution.py:35
  193.8 4.2 %all-to-all-start.3 = ((f32[8,4,256]{2,1,0:T(4,128)}), f32[8,4,256]{2,1,0:T(4,128)S(1)}, u32[]{:S(2)}, u32[]{:S(2)}) async-start(f32[8,4,256]{2,1,0:T(4,128)} %broadcast_in_dim.43), calls=%async_computation.3 | async-start | bytes 65536 | tf_op jit(solution)/shard_map/all_to_all | solution.py:35
  198.8 4.1 %all-to-all-done.3 = f32[8,4,256]{2,1,0:T(4,128)S(1)} async-done(((f32[8,4,256]{2,1,0:T(4,128)}), f32[8,4,256]{2,1,0:T(4,128)S(1)}, u32[]{:S(2)}, u32[]{:S(2)}) %all-to-all-start.3) | async-done | bytes 32800 | tf_op jit(solution)/shard_map/all_to_all | solution.py:35
  204.2 4.9 %all-to-all-start.4 = ((bf16[8,256,320]{1,2,0:T(8,128)(2,1)}), bf16[8,256,320]{1,2,0:T(8,128)(2,1)S(1)}, u32[]{:S(2)}, u32[]{:S(2)}) async-start(bf16[8,256,320]{1,2,0:T(8,128)(2,1)} %broadcast_in_dim.44), calls=%async_computation.4 | async-start | bytes 2621440 | tf_op jit(solution)/shard_map/all_to_all | solution.py:35
  209.9 15.3 %all-to-all-done.4 = bf16[8,256,320]{1,2,0:T(8,128)(2,1)S(1)} async-done(((bf16[8,256,320]{1,2,0:T(8,128)(2,1)}), bf16[8,256,320]{1,2,0:T(8,128)(2,1)S(1)}, u32[]{:S(2)}, u32[]{:S(2)}) %all-to-all-start.4) | async-done | bytes 1310752 | tf_op jit(solution)/shard_map/all_to_all | solution.py:35
  225.2 4.8 %fusion.62 = f32[256,1280]{1,0:T(8,128)S(1)} fusion(bf16[256,2560]{0,1:T(8,128)(2,1)S(1)} %bitcast.72, bf16[2560,1280]{1,0:T(8,128)(2,1)} %all-gather.2.cloned.1.call-done), kind=kOutput, calls=%fused_computation.120 | convolution fusion | flops 1677721600 | bytes 9175040 | tf_op jit(solution)/shard_map/dot_general | solution.py:206
  (131 shorter events, 43.4 us)
Async XLA Ops:
  7.2 138.9 %copy-start = (bf16[2560,256]{1,0:T(8,128)(2,1)S(1)}, bf16[2560,256]{1,0:T(8,128)(2,1)}, u32[]{:S(2)}) copy-start(bf16[2560,256]{1,0:T(8,128)(2,1)} %param.13) | copy-start | bytes 3932164
  9.4 22.9 %all-to-all-start = ((bf16[8,256,320]{1,2,0:T(8,128)(2,1)}), bf16[8,256,320]{1,2,0:T(8,128)(2,1)S(1)}, u32[]{:S(2)}, u32[]{:S(2)}) async-start(bf16[8,256,320]{1,2,0:T(8,128)(2,1)} %broadcast_in_dim.36), calls=%async_computation | async-start | bytes 2621440 | tf_op jit(solution)/shard_map/all_to_all | solution.py:35
  15.2 210.0 %all-gather.2.cloned.1.call-start = ((), (), s32[]{:S(2)}) async-start(), calls=%async_computation.5 | async-start | bytes 6656000 | tf_op jit(solution)/shard_map/all_gather | solution.py:203
  18.4 19.0 %copy-start.10 = (f32[2560]{0:T(1024)S(1)}, f32[2560]{0:T(1024)}, u32[]{:S(2)}) copy-start(f32[2560]{0:T(1024)} %param.17) | copy-start | bytes 30724
  32.3 137.9 %all-to-all-start.2 = ((bf16[256,8,320]{0,2,1:T(8,128)(2,1)}), bf16[256,8,320]{0,2,1:T(8,128)(2,1)}, u32[]{:S(2)}, u32[]{:S(2)}) async-start(bf16[256,8,320]{0,2,1:T(8,128)(2,1)} %bitcast.73), calls=%async_computation.2 | async-start | bytes 2621440 | tf_op jit(solution)/shard_map/all_to_all | solution.py:95
  38.9 17.1 %copy-start.17 = (f32[256]{0:T(256)S(1)}, f32[256]{0:T(256)}, u32[]{:S(2)}) copy-start(f32[256]{0:T(256)} %param.21) | copy-start | bytes 3076
  39.6 16.3 %collective-permute-start = (bf16[256,256]{0,1:T(8,128)(2,1)S(1)}, bf16[256,256]{0,1:T(8,128)(2,1)S(1)}, u32[]{:S(2)}, u32[]{:S(2)}) collective-permute-start(bf16[256,256]{0,1:T(8,128)(2,1)S(1)} %convolution_convert_fusion), channel_id=1, source_target_pairs={{0,64},{64,0},{128,192},{192,128},{1,65},{65,1},{129,193},{193,129... | collective-permute-start | bytes 393224 | tf_op jit(solution)/shard_map/ppermute | solution.py:17
  43.0 14.3 %copy-start.13 = (f32[128]{0:T(128)}, f32[128]{0:T(128)S(1)}, u32[]{:S(2)}) copy-start(f32[128]{0:T(128)S(1)} %negate_power_fusion) | copy-start | bytes 1540
  57.3 47.9 %collective-permute-start.1 = (bf16[2,256,256]{1,2,0:T(8,128)(2,1)S(1)}, bf16[2,256,256]{1,2,0:T(8,128)(2,1)S(1)}, u32[]{:S(2)}, u32[]{:S(2)}) collective-permute-start(bf16[2,256,256]{1,2,0:T(8,128)(2,1)S(1)} %pad_maximum_fusion.1), channel_id=1, source_target_pairs={{0,2},{1,3},{2,4},{3,5},{4,6},{5,7},{6,8},{7,9},{8,10},{9,11},{10,... | collective-permute-start | bytes 786440 | tf_op jit(solution)/shard_map/ppermute | solution.py:23
  59.3 48.7 %collective-permute-start.2 = (bf16[2,256,256]{1,2,0:T(8,128)(2,1)S(1)}, bf16[2,256,256]{1,2,0:T(8,128)(2,1)}, u32[]{:S(2)}, u32[]{:S(2)}) collective-permute-start(bf16[2,256,256]{1,2,0:T(8,128)(2,1)S(1)} %pad_maximum_fusion.1), channel_id=1, source_target_pairs={{0,4},{1,5},{2,6},{3,7},{4,8},{5,9},{6,10},{7,11},{8,12},{9,13},{1... | collective-permute-start | bytes 786440 | tf_op jit(solution)/shard_map/ppermute | solution.py:23
  65.4 39.9 %collective-permute-start.3 = (bf16[2,256,256]{1,2,0:T(8,128)(2,1)S(1)}, bf16[2,256,256]{1,2,0:T(8,128)(2,1)S(1)}, u32[]{:S(2)}, u32[]{:S(2)}) collective-permute-start(bf16[2,256,256]{1,2,0:T(8,128)(2,1)S(1)} %pad_maximum_fusion.1), channel_id=1, source_target_pairs={{0,6},{1,7},{2,8},{3,9},{4,10},{5,11},{6,12},{7,13},{8,14},{9,15},... | collective-permute-start | bytes 786440 | tf_op jit(solution)/shard_map/ppermute | solution.py:23
  67.4 45.6 %collective-permute-start.4 = (bf16[2,256,256]{1,2,0:T(8,128)(2,1)S(1)}, bf16[2,256,256]{1,2,0:T(8,128)(2,1)S(1)}, u32[]{:S(2)}, u32[]{:S(2)}) collective-permute-start(bf16[2,256,256]{1,2,0:T(8,128)(2,1)S(1)} %pad_maximum_fusion.1), channel_id=1, source_target_pairs={{0,8},{1,9},{2,10},{3,11},{4,12},{5,13},{6,14},{7,15},{8,16},{9,17... | collective-permute-start | bytes 786440 | tf_op jit(solution)/shard_map/ppermute | solution.py:23
  69.3 73.3 %collective-permute-start.7 = (bf16[2,256,256]{1,2,0:T(8,128)(2,1)S(1)}, bf16[2,256,256]{1,2,0:T(8,128)(2,1)S(1)}, u32[]{:S(2)}, u32[]{:S(2)}) collective-permute-start(bf16[2,256,256]{1,2,0:T(8,128)(2,1)S(1)} %pad_maximum_fusion.1), channel_id=1, source_target_pairs={{0,16},{1,17},{2,18},{3,19},{4,20},{5,21},{6,22},{7,23},{8,24},{9,... | collective-permute-start | bytes 786440 | tf_op jit(solution)/shard_map/ppermute | solution.py:23
  105.3 39.9 %copy-start.16 = (s32[9]{0:T(128)S(1)}, s32[9]{0:T(128)}, u32[]{:S(2)}) copy-start(s32[9]{0:T(128)} %get-tuple-element.38) | copy-start | bytes 112
  105.3 40.7 %copy-start.3 = (bf16[256,2560]{0,1:T(8,128)(2,1)S(1)}, bf16[256,2560]{0,1:T(8,128)(2,1)}, u32[]{:S(2)}) copy-start(bf16[256,2560]{0,1:T(8,128)(2,1)} %copy-done.2) | copy-start | bytes 3932164
  105.3 30.4 %collective-permute-start.5 = (bf16[2,2,256,256]{2,3,1,0:T(8,128)(2,1)S(1)}, bf16[2,2,256,256]{2,3,1,0:T(8,128)(2,1)S(1)}, u32[]{:S(2)}, u32[]{:S(2)}) collective-permute-start(bf16[2,2,256,256]{2,3,1,0:T(8,128)(2,1)S(1)} %pad_maximum_fusion), channel_id=1, source_target_pairs={{0,8},{1,9},{2,10},{3,11},{4,12},{5,13},{6,14},{7,15},{8,16},{9,17... | collective-permute-start | bytes 1572872 | tf_op jit(solution)/shard_map/ppermute | solution.py:23
  108.0 33.1 %collective-permute-start.6 = (bf16[2,256,256]{1,2,0:T(8,128)(2,1)}, bf16[2,256,256]{1,2,0:T(8,128)(2,1)S(1)}, u32[]{:S(2)}, u32[]{:S(2)}) collective-permute-start(bf16[2,256,256]{1,2,0:T(8,128)(2,1)} %collective-permute-done.2), channel_id=1, source_target_pairs={{0,8},{1,9},{2,10},{3,11},{4,12},{5,13},{6,14},{7,15},{8,16},{9,17... | collective-permute-start | bytes 786440 | tf_op jit(solution)/shard_map/ppermute | solution.py:23
  136.4 10.3 %copy-start.18 = (f32[256]{0:T(256)S(1)}, f32[256]{0:T(256)}, u32[]{:S(2)}) copy-start(f32[256]{0:T(256)} %param.20) | copy-start | bytes 3076
  143.3 14.5 %collective-permute-start.8 = (bf16[9,2,256,256]{2,3,1,0:T(8,128)(2,1)}, bf16[9,2,256,256]{2,3,1,0:T(8,128)(2,1)}, u32[]{:S(2)}, u32[]{:S(2)}) collective-permute-start(bf16[9,2,256,256]{2,3,1,0:T(8,128)(2,1)} %bitcast_dynamic-update-slice_fusion), channel_id=1, source_target_pairs={{0,1},{1,0},{2,3},{3,2},{4,5},{5,4},{6,7},{7,6},{8,9},{9,8},{10,11... | collective-permute-start | bytes 7077896 | tf_op jit(solution)/shard_map/ppermute | solution.py:17
  170.2 21.1 %copy-start.6 = (bf16[256,320]{0,1:T(8,128)(2,1)S(1)}, bf16[256,320]{0,1:T(8,128)(2,1)}, u32[]{:S(2)}) copy-start(bf16[256,320]{0,1:T(8,128)(2,1)} %param.12) | copy-start | bytes 491524
  171.2 20.1 %all-to-all-start.1 = ((bf16[8,256,256]{2,1,0:T(8,128)(2,1)}), bf16[8,256,256]{2,1,0:T(8,128)(2,1)S(1)}, u32[]{:S(2)}, u32[]{:S(2)}) async-start(bf16[8,256,256]{2,1,0:T(8,128)(2,1)} %broadcast_in_dim.42), calls=%async_computation.1 | async-start | bytes 2097152 | tf_op jit(solution)/shard_map/all_to_all | solution.py:35
  193.8 9.0 %all-to-all-start.3 = ((f32[8,4,256]{2,1,0:T(4,128)}), f32[8,4,256]{2,1,0:T(4,128)S(1)}, u32[]{:S(2)}, u32[]{:S(2)}) async-start(f32[8,4,256]{2,1,0:T(4,128)} %broadcast_in_dim.43), calls=%async_computation.3 | async-start | bytes 65536 | tf_op jit(solution)/shard_map/all_to_all | solution.py:35
  204.2 21.1 %all-to-all-start.4 = ((bf16[8,256,320]{1,2,0:T(8,128)(2,1)}), bf16[8,256,320]{1,2,0:T(8,128)(2,1)S(1)}, u32[]{:S(2)}, u32[]{:S(2)}) async-start(bf16[8,256,320]{1,2,0:T(8,128)(2,1)} %broadcast_in_dim.44), calls=%async_computation.4 | async-start | bytes 2621440 | tf_op jit(solution)/shard_map/all_to_all | solution.py:35
  209.9 20.1 %copy-start.7 = (bf16[2,128,256]{2,1,0:T(8,128)(2,1)}, bf16[2,128,256]{2,1,0:T(8,128)(2,1)S(1)}, u32[]{:S(2)}) copy-start(bf16[2,128,256]{2,1,0:T(8,128)(2,1)S(1)} %scatter_fusion) | copy-start | bytes 393220
  (15 other events, 52.0 us)
Sparse Core Ops, SparseCore 0:
  19.9 114.9 all-gather.1
